TPU v7x, 256 devices: a whole 4x4x8 slice. The times are simulated.
256 devices in a mesh: tok: 32 (over z, x), head: 8 (over y, core).
Axes of the slice: x: 4, y: 4, z: 8, core: 2. Of those that a mesh axis runs over, the one named last changes fastest.
Arguments:
- embeddings: bfloat16 [4096, 4096], P('tok'), may hold values from -6 to 6
- norm_gain: bfloat16 [4096], replicated, may hold values from 0.099609375 to 1.8984375
- query_key_value_weight: bfloat16 [4096, 6144], P(None, 'head'), may hold values from -0.09375 to 0.09375
- embed_table: bfloat16 [65536, 4096], P('tok', 'head'), may hold values from -6 to 6
- rotated_cache_pages: bfloat16 [32, 32, 256, 2048], P('tok', None, None, 'head'), may hold values from -300 to 300
- page_owner_device: int32 [32, 32], P('tok'), may hold values from 0 to 31, each once within a row
- cached_length: int32 [32], P('tok'), may hold values from 2 to 8192, as said below
- vocab_shard: int32 [4096, 1], P('tok'), may hold values from 0 to 31; in each aligned block of 128 rows (0 to 127, 128 to 255, ...) at most 8 rows name the same one
- shard_row: int32 [4096], P('tok'), may hold values from 0 to 2047
- accept: int32 [4096], P('tok'), may hold values from 0 to 1, as said below
Outputs:
- out_first: bfloat16 [4096, 4096], P('tok', 'head')
- out_second: bfloat16 [4096, 4096], P('tok', 'head')
Inputs may be any that keep to these rules, and one draw needn't show every extreme that they name: `page_owner_device`: each row names every device of the tok axis once. `cached_length`: some request has exactly 8192 cached positions. `vocab_shard`: at most 8 of the 128 tokens of one request name the same shard, and some shard is named that often. `accept`: at most 32 accepted tokens in one request's block; some block has exactly 32.
All inputs are finite; a program needn't handle non-finite values.
Results may differ from a plain program's by a relative error of at most 0.017.
The roundings to bfloat16 on the way count: a program that leaves them out, or rounds other values in their place, can miss the bound.
Values may be sent and summed in bfloat16 or wider, within the bound.
No kernel may reach another device: no remote copies, remote signals or barrier semaphores. Data moves between devices by JAX's collectives and lax.ppermute only.
A program may use at most 128 MiB of HBM per device.

v0:
```python
import math

import jax
import jax.numpy as jnp
from jax import lax
from jax.sharding import PartitionSpec as P

QUERY_HEADS = 32
KEY_VALUE_HEADS = 8
HEAD_SIZE = 128


THETA = 500000.0


def angles(positions):
    steps_half = jnp.arange(HEAD_SIZE // 2, dtype=jnp.float32)
    frequency = THETA ** (-(steps_half * 2.0) / HEAD_SIZE)
    return positions.astype(jnp.float32)[:, None] * frequency[None, :]


def rotate(vectors, turning):
    half_width = vectors.shape[-1] // 2
    former = vectors[..., :half_width]
    latter = vectors[..., half_width:]
    cosine = jnp.cos(turning)
    sine_of = jnp.sin(turning)
    return jnp.concatenate(
        [former * cosine - latter * sine_of, latter * cosine + former * sine_of], axis=-1
    )


def project(inputs, norm_gain, query_key_value_weight, positions):
    widened = inputs.astype(jnp.float32)
    inverse = lax.rsqrt(jnp.mean(widened * widened, axis=-1, keepdims=True) + 1e-05)
    normed = (widened * inverse * norm_gain.astype(jnp.float32)).astype(jnp.bfloat16)
    combined = jnp.dot(normed, query_key_value_weight, preferred_element_type=jnp.float32)
    heads_per_group = QUERY_HEADS // KEY_VALUE_HEADS
    combined = combined.reshape(inputs.shape[0], -1, heads_per_group + 2, HEAD_SIZE)
    turning = angles(positions)[:, None, None, :]
    query_vectors = rotate(combined[:, :, :heads_per_group], turning).astype(jnp.bfloat16)
    block_keys = rotate(combined[:, :, heads_per_group : heads_per_group + 1], turning)[
        :, :, 0
    ].astype(jnp.bfloat16)
    block_values = combined[:, :, heads_per_group + 1].astype(jnp.bfloat16)
    return (query_vectors, block_keys, block_values)


def attend(query_vectors, block_keys, block_values, page_keys, page_values, usable):
    factor = 1.0 / math.sqrt(HEAD_SIZE)
    scores_cache = (
        jnp.einsum("bgqd,kgd->gqbk", query_vectors, page_keys, preferred_element_type=jnp.float32)
        * factor
    )
    scores_cache = jnp.where(usable[None, None, None, :], scores_cache, -1e30)
    scores_block = (
        jnp.einsum("bgqd,cgd->gqbc", query_vectors, block_keys, preferred_element_type=jnp.float32)
        * factor
    )
    highest = jnp.maximum(jnp.max(scores_cache, axis=-1), jnp.max(scores_block, axis=-1))[..., None]
    exp_cache = jnp.exp(scores_cache - highest)
    exp_block = jnp.exp(scores_block - highest)
    totals = jnp.sum(exp_cache, axis=-1) + jnp.sum(exp_block, axis=-1)
    weights_cache = exp_cache.astype(jnp.bfloat16)
    weights_block = exp_block.astype(jnp.bfloat16)
    combined = jnp.einsum(
        "gqbk,kgd->bgqd", weights_cache, page_values, preferred_element_type=jnp.float32
    )
    combined = combined + jnp.einsum(
        "gqbc,cgd->bgqd", weights_block, block_values, preferred_element_type=jnp.float32
    )
    result = combined / jnp.transpose(totals, (2, 0, 1))[..., None]
    return result.astype(jnp.bfloat16).reshape(query_vectors.shape[0], -1)


def body(
    embeddings,
    norm_gain,
    query_key_value_weight,
    embed_table,
    rotated_cache_pages,
    page_owner_device,
    cached_length,
    vocab_shard,
    shard_row,
    accept,
):
    members = lax.axis_size("tok")
    length = embeddings.shape[0]
    sources = jnp.arange(members, dtype=jnp.int32)
    positions = cached_length[0] + jnp.arange(length, dtype=jnp.int32)
    query_vectors, block_keys, block_values = project(
        embeddings, norm_gain, query_key_value_weight, positions
    )
    arrived = lax.all_to_all(rotated_cache_pages, "tok", split_axis=1, concat_axis=0, tiled=True)
    page_size = arrived.shape[2]
    arrived = arrived.reshape(members * page_size, -1, 2, HEAD_SIZE)
    page_index = jnp.sum(
        jnp.where(page_owner_device[0][:, None] == sources[None, :], sources[:, None], 0), axis=0
    )
    page_spots = page_index[:, None] * page_size + jnp.arange(page_size, dtype=jnp.int32)[None, :]
    usable = page_spots.reshape(-1) < cached_length[0]
    page_keys = arrived[:, :, 0]
    page_values = arrived[:, :, 1]

    def run_attention(query_rows, key_rows, value_rows):
        return attend(query_rows, key_rows, value_rows, page_keys, page_values, usable)

    output_one = run_attention(query_vectors, block_keys, block_values)
    target_shard = vocab_shard[:, 0]
    capacity = max(2, 2 * length // members)
    chosen = (target_shard[:, None] == sources[None, :]).astype(jnp.int32)
    earlier = (jnp.arange(length)[:, None] > jnp.arange(length)[None, :]).astype(jnp.int32)
    slot_rank = jnp.sum(jnp.dot(earlier, chosen) * chosen, axis=1)
    wanted = jnp.zeros((members, capacity), jnp.int32).at[target_shard, slot_rank].set(shard_row)
    found_rows = jnp.take(
        embed_table, lax.all_to_all(wanted, "tok", split_axis=0, concat_axis=0, tiled=True), axis=0
    )
    returned = lax.all_to_all(found_rows, "tok", split_axis=0, concat_axis=0, tiled=True)
    replacement = returned[target_shard, slot_rank]
    full_rows = lax.all_gather(replacement, "head", axis=1, tiled=True)
    replaced = jnp.where(accept[:, None] == 1, full_rows, embeddings)
    queries_two, keys_two, values_two = project(
        replaced, norm_gain, query_key_value_weight, positions
    )
    output_two = run_attention(queries_two, keys_two, values_two)
    return (output_one, output_two)


def solution(mesh):
    return jax.shard_map(
        body,
        mesh=mesh,
        in_specs=(
            P("tok", None),
            P(),
            P(None, "head"),
            P("tok", "head"),
            P("tok", None, None, "head"),
            P("tok", None),
            P("tok"),
            P("tok", None),
            P("tok"),
            P("tok"),
        ),
        out_specs=(P("tok", "head"), P("tok", "head")),
        check_vma=False,
    )
```

profile of v0, /device:TPU:28, one launch (start us, length us, event | category | flops | bytes accessed | tf_op | source)
XLA Modules:
  0.0 241.9 jit_solution(14365437352633551345)
XLA Ops:
  7.2 0.0 copy-start
  7.2 1.0 fusion.36
  8.2 0.7 fusion.89
  8.8 10.9 %scatter_fusion = s32[32,8]{0,1:T(8,128)S(1)} fusion(s32[32,8]{0,1:T(8,128)S(1)} %broadcast_in_dim.55, s32[128]{0:T(128)S(1)} %get-tuple-element.14, s32[128]{0:T(128)} %param.18), kind=kCustom, calls=%fused_computation.2 | custom fusion | bytes 2560 | tf_op jit(solution)/shard_map/scatter | solution.py:115
  19.8 0.1 copy.91
  19.9 19.1 %all_to_all.29 = s32[32,1,8]{2,1,0:T(1,128)S(1)} all-to-all(s32[32,1,8]{2,1,0:T(1,128)S(1)} %copy.91), channel_id=1, replica_groups=mesh['tok'=32,'head'=8] {'tok'}, dimensions={0} | all-to-all | bytes 2048 | tf_op jit(solution)/shard_map/all_to_all | solution.py:117
  38.9 0.1 reshape.410
  39.0 0.1 copy.92
  39.1 0.1 copy.93
  39.2 0.0 copy-done
  39.2 0.0 copy-start.6
  39.2 0.0 copy-start.7
  39.2 0.0 copy-start.8
  39.2 0.0 copy-start.3
  39.3 1.2 gather_fusion
  40.4 0.1 bitcast_select_fusion.2
  40.5 15.1 %all_to_all.30 = bf16[32,8,512]{2,1,0:T(8,128)(2,1)S(1)} all-to-all(bf16[32,8,512]{2,1,0:T(8,128)(2,1)S(1)} %bitcast_select_fusion.2), channel_id=1, replica_groups=mesh['tok'=32,'head'=8] {'tok'}, dimensions={0} | all-to-all | bytes 524288 | tf_op jit(solution)/shard_map/all_to_all | solution.py:119
  55.6 6.6 %all-to-all-start = ((bf16[1,32,256,256]{3,2,0,1:T(8,128)(2,1)}), bf16[1,32,256,256]{3,2,0,1:T(8,128)(2,1)}, u32[]{:S(2)}, u32[]{:S(2)}) async-start(bf16[1,32,256,256]{3,2,0,1:T(8,128)(2,1)} %bitcast.163), calls=%async_computation | async-start | bytes 8388608 | tf_op jit(solution)/shard_map/all_to_all | solution.py:95
  62.2 0.0 all-gather.2.cloned.1.call-start
  62.3 1.9 gather_fusion.1
  64.2 0.0 all-gather.2.cloned.1.call-update
  64.3 0.0 copy-done.6
  64.9 0.0 copy-done.7
  64.9 0.1 select_reduce_fusion
  65.0 0.1 add_compare_fusion
  65.2 0.0 copy-done.8
  65.2 0.3 multiply_cosine_fusion
  65.5 25.1 %all-gather.2.cloned.1.call-done = bf16[128,4096]{1,0:T(8,128)(2,1)} async-done(((bf16[128,512]{1,0:T(8,128)(2,1)}), bf16[128,4096]{1,0:T(8,128)(2,1)}) %all-gather.2.cloned.1.call-update) | async-done | bytes 1048592 | tf_op jit(solution)/shard_map/all_gather | solution.py:121
  90.6 0.0 copy-done.3
  90.6 1.9 fusion.17
  92.5 5.8 %fusion.41 = f32[128,768]{0,1:T(8,128)S(1)} fusion(bf16[4096,768]{1,0:T(8,128)(2,1)} %param.12, f32[128]{0:T(128)S(1)} %get-tuple-element.44, f32[4096]{0:T(1024)S(1)} %convert_element_type.83, bf16[128,4096]{1,0:T(8,128)(2,1)} %all-gather.2.cloned.1.call-done, bf16[128,4096]{1,0:T(8,128)(2,1)S(1)} %copy-done.3, pred[128]{0:T(512)(128)(4,1)S(1)} %broadcast_compare_fusion), kind=kOutput, calls=%fused_computation.48 | convolution fusion | flops 807927808 | bytes 8798848 | tf_op jit(solution)/shard_map/dot_general | solution.py:37
  98.3 0.0 copy-start.4
  98.3 0.1 copy.116
  98.5 0.1 copy.115
  98.6 5.4 %fusion.43 = f32[128,768]{0,1:T(8,128)S(1)} fusion(bf16[4096,768]{1,0:T(8,128)(2,1)} %param.12, bf16[128,4096]{1,0:T(8,128)(2,1)S(1)} %copy-done.3, f32[4096]{0:T(1024)S(1)} %convert_element_type.83, f32[128]{0:T(128)S(1)} %get-tuple-element.45), kind=kOutput, calls=%fused_computation.49 | convolution fusion | flops 807403520 | bytes 7750144 | tf_op jit(solution)/shard_map/dot_general | solution.py:37
  104.0 0.1 copy.111
  104.2 0.1 copy.112
  104.3 0.2 fusion.76
  104.5 0.1 fusion.59
  104.7 0.3 fusion.99
  105.0 0.0 copy-done.4
  105.0 0.3 fusion.101
  105.3 50.1 %all-to-all-done = bf16[1,32,256,256]{3,2,0,1:T(8,128)(2,1)} async-done(((bf16[1,32,256,256]{3,2,0,1:T(8,128)(2,1)}), bf16[1,32,256,256]{3,2,0,1:T(8,128)(2,1)}, u32[]{:S(2)}, u32[]{:S(2)}) %all-to-all-start) | async-done | bytes 4194336 | tf_op jit(solution)/shard_map/all_to_all | solution.py:95
  155.3 6.9 %reshape.435 = bf16[8192,1,2,128]{3,2,0,1:T(2,128)(2,1)} reshape(bf16[1,32,256,256]{3,2,0,1:T(8,128)(2,1)} %all-to-all-done) | data formatting | bytes 8388608 | tf_op jit(solution)/shard_map/reshape | solution.py:97
  162.3 9.8 %fusion.95 = (bf16[8192,1,1,128]{3,2,0,1:T(2,128)(2,1)S(1)}, bf16[8192,1,1,128]{3,2,0,1:T(2,128)(2,1)}) fusion(bf16[8192,1,2,128]{3,2,0,1:T(2,128)(2,1)} %reshape.435), kind=kLoop, calls=%fused_computation.135 | loop fusion | bytes 8388608 | tf_op jit(solution)/shard_map/slice | solution.py:103
  172.1 8.2 %fusion.98 = (f32[4,128]{1,0:T(4,128)}, f32[1,4,128,8192]{3,2,1,0:T(8,128)}) fusion(bf16[8192,1,1,128]{3,2,0,1:T(2,128)(2,1)S(1)} %get-tuple-element.16, bf16[128,4,64]{2,0,1:T(8,128)(2,1)S(1)} %get-tuple-element.30, bf16[128,4,64]{2,0,1:T(8,128)(2,1)S(1)} %get-tuple-element.31, pred[8192]{0:T(1024)(128)(4,1)S(1)} %lt.48), kind=kOutput, calls=%fused_computation.138 | convolution fusion | flops 1086586368 | bytes 19015680 | tf_op jit(solution)/shard_map/bgqd,kgd->gqbk/dot_general | solution.py:52
  180.3 7.7 %fusion.100 = (f32[4,128]{1,0:T(4,128)S(1)}, f32[1,4,128,8192]{3,2,1,0:T(8,128)}) fusion(bf16[8192,1,1,128]{3,2,0,1:T(2,128)(2,1)S(1)} %get-tuple-element.16, bf16[128,4,64]{2,0,1:T(8,128)(2,1)S(1)} %get-tuple-element.19, bf16[128,4,64]{2,0,1:T(8,128)(2,1)S(1)} %get-tuple-element.18, pred[8192]{0:T(1024)(128)(4,1)S(1)} %lt.48), kind=kOutput, calls=%fused_computation.140 | convolution fusion | flops 1086586368 | bytes 19015680 | tf_op jit(solution)/shard_map/bgqd,kgd->gqbk/dot_general | solution.py:52
  188.0 0.0 copy-start.5
  188.0 8.3 %copy.114 = bf16[8192,1,1,128]{0,3,2,1:T(8,128)(2,1)S(1)} copy(bf16[8192,1,1,128]{3,2,0,1:T(2,128)(2,1)} %get-tuple-element.17) | data formatting | bytes 4194304
  196.3 0.0 copy-start.2
  196.4 0.0 copy-done.5
  196.4 8.9 %fusion.2 = f32[4,128]{1,0:T(4,128)S(1)} fusion(f32[1,4,128,8192]{3,2,1,0:T(8,128)} %get-tuple-element.37, f32[4,128]{1,0:T(4,128)S(1)} %max.18), kind=kLoop, calls=%fused_computation.9 | loop fusion | flops 8388096 | bytes 16781312 | tf_op jit(solution)/shard_map/reduce_sum | solution.py:63
  205.2 0.0 copy-done.2
  205.2 8.8 %fusion.26 = f32[128,4,128]{2,0,1:T(8,128)S(1)} fusion(bf16[8192,1,1,128]{0,3,2,1:T(8,128)(2,1)S(1)} %copy.114, f32[1,4,128,8192]{3,2,1,0:T(8,128)} %get-tuple-element.37, f32[4,128]{1,0:T(4,128)S(1)} %max.18), kind=kOutput, calls=%fused_computation.40 | convolution fusion | flops 1082130432 | bytes 19138560 | tf_op jit(solution)/shard_map/gqbk,kgd->bgqd/dot_general | solution.py:66
  214.0 0.0 copy-start.1
  214.0 8.4 %fusion.31 = f32[128,4,128]{2,0,1:T(8,128)S(1)} fusion(bf16[8192,1,1,128]{0,3,2,1:T(8,128)(2,1)} %copy-done.2, f32[1,4,128,8192]{3,2,1,0:T(8,128)} %get-tuple-element.41, f32[4,128]{1,0:T(4,128)S(1)} %max.19), kind=kOutput, calls=%fused_computation.41 | convolution fusion | flops 1082130432 | bytes 19138560 | tf_op jit(solution)/shard_map/gqbk,kgd->bgqd/dot_general | solution.py:66
  222.4 8.1 %fusion.4 = f32[4,128]{1,0:T(4,128)S(1)} fusion(f32[1,4,128,8192]{3,2,1,0:T(8,128)} %get-tuple-element.41, f32[4,128]{1,0:T(4,128)S(1)} %max.19), kind=kLoop, calls=%fused_computation.11 | loop fusion | flops 8388096 | bytes 16781312 | tf_op jit(solution)/shard_map/reduce_sum | solution.py:63
  230.5 0.1 fusion.49
  230.6 0.9 fusion.38
  231.5 1.7 copy.99
  233.1 0.1 fusion.51
  233.2 1.0 fusion.40
  234.3 0.8 copy.100
  235.0 0.0 copy-done.1
  (17 shorter events, 0.1 us)
Async XLA Ops:
  7.2 32.0 %copy-start = (bf16[2048,512]{1,0:T(8,128)(2,1)S(1)}, bf16[2048,512]{1,0:T(8,128)(2,1)}, u32[]{:S(2)}) copy-start(bf16[2048,512]{1,0:T(8,128)(2,1)} %param.13) | copy-start | bytes 6291460
  39.2 25.1 %copy-start.6 = (bf16[4096]{0:T(1024)(128)(2,1)S(1)}, bf16[4096]{0:T(1024)(128)(2,1)}, u32[]{:S(2)}) copy-start(bf16[4096]{0:T(1024)(128)(2,1)} %param.11) | copy-start | bytes 24580
  39.2 25.7 %copy-start.7 = (s32[1,32]{1,0:T(1,128)S(1)}, s32[1,32]{1,0:T(1,128)}, u32[]{:S(2)}) copy-start(s32[1,32]{1,0:T(1,128)} %param.15) | copy-start | bytes 388
  39.2 25.9 %copy-start.8 = (s32[128]{0:T(128)S(1)}, s32[128]{0:T(128)}, u32[]{:S(2)}) copy-start(s32[128]{0:T(128)} %param.19) | copy-start | bytes 1540
  39.2 51.4 %copy-start.3 = (bf16[128,4096]{1,0:T(8,128)(2,1)S(1)}, bf16[128,4096]{1,0:T(8,128)(2,1)}, u32[]{:S(2)}) copy-start(bf16[128,4096]{1,0:T(8,128)(2,1)} %param.10) | copy-start | bytes 3145732
  55.6 99.7 %all-to-all-start = ((bf16[1,32,256,256]{3,2,0,1:T(8,128)(2,1)}), bf16[1,32,256,256]{3,2,0,1:T(8,128)(2,1)}, u32[]{:S(2)}, u32[]{:S(2)}) async-start(bf16[1,32,256,256]{3,2,0,1:T(8,128)(2,1)} %bitcast.163), calls=%async_computation | async-start | bytes 8388608 | tf_op jit(solution)/shard_map/all_to_all | solution.py:95
  62.2 28.4 %all-gather.2.cloned.1.call-start = ((), (), s32[]{:S(2)}) async-start(), calls=%async_computation.3 | async-start | bytes 1179648 | tf_op jit(solution)/shard_map/all_gather | solution.py:121
  98.3 6.7 %copy-start.4 = (f32[128,768]{0,1:T(8,128)}, f32[128,768]{0,1:T(8,128)S(1)}, u32[]{:S(2)}) copy-start(f32[128,768]{0,1:T(8,128)S(1)} %fusion.41) | copy-start | bytes 1179652
  188.0 8.4 %copy-start.5 = (f32[4,128]{1,0:T(4,128)S(1)}, f32[4,128]{1,0:T(4,128)}, u32[]{:S(2)}) copy-start(f32[4,128]{1,0:T(4,128)} %get-tuple-element.36) | copy-start | bytes 6148
  196.3 8.9 %copy-start.2 = (bf16[8192,1,1,128]{0,3,2,1:T(8,128)(2,1)}, bf16[8192,1,1,128]{0,3,2,1:T(8,128)(2,1)S(1)}, u32[]{:S(2)}) copy-start(bf16[8192,1,1,128]{0,3,2,1:T(8,128)(2,1)S(1)} %copy.114) | copy-start | bytes 6291460
  214.0 21.0 %copy-start.1 = (bf16[2048,512]{1,0:T(8,128)(2,1)S(1)}, bf16[2048,512]{1,0:T(8,128)(2,1)}, u32[]{:S(2)}) copy-start(bf16[2048,512]{1,0:T(8,128)(2,1)} %param.13) | copy-start | bytes 6291460
Sparse Core Ops, SparseCore 0:
  65.5 25.0 all-gather.1
where the time goes:
time: 243 us; the launch traced here: 242 us
  waiting for transfers between devices  75.2 us (31%)
  matrix products  47.7 us (20%)
  local copies, waits for them, and re-layouts  42.5 us (17%)
  blocking collectives  34.2 us (14%)
  other arithmetic  20.6 us (8%)
  between operations  15 us (6%)
  starting transfers between devices  6.66 us (3%)
    all_to_all x1, waiting for transfers between devices, body(): lax.all_to_all(rotated_cache_pages, 'tok', split_axis=1, concat_axis=0, t...  50.1 us
    all_gather x1, waiting for transfers between devices, body(): full_rows = lax.all_gather(replacement, 'head', axis=1, tiled=True)  25.1 us
    all_to_all x1, blocking collectives, body(): lax.all_to_all(wanted, 'tok', split_axis=0, concat_axis=0, tiled=True)  19.1 us
    dot_general x2, matrix products, attend(): jnp.einsum('gqbk,kgd->bgqd', weights_cache, page_values, preferred_elemen...  17.1 us
    reduce_sum x4, other arithmetic, attend(): totals = jnp.sum(exp_cache, axis=-1) + jnp.sum(exp_block, axis=-1)  17.1 us
    dot_general x2, matrix products, attend(): jnp.einsum('bgqd,kgd->gqbk', query_vectors, page_keys, preferred_element_...  15.9 us
    all_to_all x1, blocking collectives, body(): lax.all_to_all(found_rows, 'tok', split_axis=0, concat_axis=0, tiled=True)  15.1 us
    unnamed x25, local copies, waits for them, and re-layouts  11.3 us
  transfers between devices with their start and end apart: 2, of which 2 were waited for; matrix products, arithmetic and copies ran while one was open for 7% of the time, Pallas kernels for 0%

commit v1 on v0

v1 whole, which is shorter than its diff:
```python
import math

import jax
import jax.numpy as jnp
from jax import lax
from jax.experimental import pallas as pl
from jax.experimental.pallas import tpu as pltpu
from jax.sharding import PartitionSpec as P

QUERY_HEADS = 32
KEY_VALUE_HEADS = 8
HEAD_SIZE = 128
HEADS_PER_GROUP = QUERY_HEADS // KEY_VALUE_HEADS


THETA = 500000.0
KEY_CHUNK = 1024


def angles(positions):
    steps_half = jnp.arange(HEAD_SIZE // 2, dtype=jnp.float32)
    frequency = THETA ** (-(steps_half * 2.0) / HEAD_SIZE)
    return positions.astype(jnp.float32)[:, None] * frequency[None, :]


def rotate(vectors, turning):
    half_width = vectors.shape[-1] // 2
    former = vectors[..., :half_width]
    latter = vectors[..., half_width:]
    cosine = jnp.cos(turning)
    sine_of = jnp.sin(turning)
    return jnp.concatenate(
        [former * cosine - latter * sine_of, latter * cosine + former * sine_of], axis=-1
    )


def project(inputs, norm_gain, query_key_value_weight, positions):
    widened = inputs.astype(jnp.float32)
    inverse = lax.rsqrt(jnp.mean(widened * widened, axis=-1, keepdims=True) + 1e-05)
    normed = (widened * inverse * norm_gain.astype(jnp.float32)).astype(jnp.bfloat16)
    combined = jnp.dot(normed, query_key_value_weight, preferred_element_type=jnp.float32)
    rows = inputs.shape[0]
    combined = combined.reshape(rows, -1, HEADS_PER_GROUP + 2, HEAD_SIZE)
    turning = angles(positions)[:, None, None, :]
    query_vectors = rotate(combined[:, :, :HEADS_PER_GROUP], turning).astype(jnp.bfloat16)
    block_keys = rotate(combined[:, :, HEADS_PER_GROUP : HEADS_PER_GROUP + 1], turning)[
        :, :, 0
    ].astype(jnp.bfloat16)
    block_values = combined[:, :, HEADS_PER_GROUP + 1].astype(jnp.bfloat16)
    return (
        query_vectors.reshape(rows, -1),
        block_keys.reshape(rows, -1),
        block_values.reshape(rows, -1),
    )


def attention_kernel(q1_ref, q2_ref, kb1_ref, vb1_ref, kb2_ref, vb2_ref, pg_ref, us_ref,
                     o1_ref, o2_ref, s_ref):
    factor = 1.0 / math.sqrt(HEAD_SIZE)
    nt = (((1,), (1,)), ((), ()))
    rows = q1_ref.shape[0]
    q = jnp.concatenate([q1_ref[...], q2_ref[...]], axis=0)
    sb1 = lax.dot_general(q1_ref[...], kb1_ref[...], nt, preferred_element_type=jnp.float32) * factor
    sb2 = lax.dot_general(q2_ref[...], kb2_ref[...], nt, preferred_element_type=jnp.float32) * factor
    high = jnp.concatenate(
        [jnp.max(sb1, axis=1, keepdims=True), jnp.max(sb2, axis=1, keepdims=True)], axis=0
    )
    keys_total = pg_ref.shape[0]
    chunks = keys_total // KEY_CHUNK
    for c in range(chunks):
        lo = c * KEY_CHUNK
        k = pg_ref[lo : lo + KEY_CHUNK, 0:HEAD_SIZE]
        sc = lax.dot_general(q, k, nt, preferred_element_type=jnp.float32) * factor
        sc = jnp.where(us_ref[:, lo : lo + KEY_CHUNK] > 0, sc, -1e30)
        s_ref[:, lo : lo + KEY_CHUNK] = sc
        high = jnp.maximum(high, jnp.max(sc, axis=1, keepdims=True))
    h1 = high[:rows]
    h2 = high[rows:]
    eb1 = jnp.exp(sb1 - h1)
    eb2 = jnp.exp(sb2 - h2)
    tot = jnp.concatenate(
        [jnp.sum(eb1, axis=1, keepdims=True), jnp.sum(eb2, axis=1, keepdims=True)], axis=0
    )
    acc = jnp.concatenate(
        [
            jnp.dot(eb1.astype(jnp.bfloat16), vb1_ref[...], preferred_element_type=jnp.float32),
            jnp.dot(eb2.astype(jnp.bfloat16), vb2_ref[...], preferred_element_type=jnp.float32),
        ],
        axis=0,
    )
    for c in range(chunks):
        lo = c * KEY_CHUNK
        e = jnp.exp(s_ref[:, lo : lo + KEY_CHUNK] - high)
        tot = tot + jnp.sum(e, axis=1, keepdims=True)
        v = pg_ref[lo : lo + KEY_CHUNK, HEAD_SIZE : 2 * HEAD_SIZE]
        acc = acc + jnp.dot(e.astype(jnp.bfloat16), v, preferred_element_type=jnp.float32)
    res = (acc / tot).astype(jnp.bfloat16)
    o1_ref[...] = res[:rows]
    o2_ref[...] = res[rows:]


def attend_both(q1, kb1, vb1, q2, kb2, vb2, pages, usable):
    rows = q1.shape[0]
    keys_total = pages.shape[0]
    qspec = pl.BlockSpec((rows, HEAD_SIZE), lambda j: (0, j))
    full = pl.BlockSpec((rows, HEAD_SIZE), lambda j: (0, 0))
    return pl.pallas_call(
        attention_kernel,
        grid=(HEADS_PER_GROUP,),
        in_specs=[
            qspec,
            qspec,
            full,
            full,
            full,
            full,
            pl.BlockSpec((keys_total, 2 * HEAD_SIZE), lambda j: (0, 0)),
            pl.BlockSpec((1, keys_total), lambda j: (0, 0)),
        ],
        out_specs=[qspec, qspec],
        out_shape=[
            jax.ShapeDtypeStruct(q1.shape, jnp.bfloat16),
            jax.ShapeDtypeStruct(q1.shape, jnp.bfloat16),
        ],
        scratch_shapes=[pltpu.VMEM((2 * rows, keys_total), jnp.float32)],
        compiler_params=pltpu.CompilerParams(vmem_limit_bytes=48 * 1024 * 1024),
    )(q1, q2, kb1, vb1, kb2, vb2, pages, usable)


def body(
    embeddings,
    norm_gain,
    query_key_value_weight,
    embed_table,
    rotated_cache_pages,
    page_owner_device,
    cached_length,
    vocab_shard,
    shard_row,
    accept,
):
    members = lax.axis_size("tok")
    length = embeddings.shape[0]
    sources = jnp.arange(members, dtype=jnp.int32)
    positions = cached_length[0] + jnp.arange(length, dtype=jnp.int32)
    arrived = lax.all_to_all(rotated_cache_pages, "tok", split_axis=1, concat_axis=0, tiled=True)
    page_size = arrived.shape[2]
    pages = arrived.reshape(members * page_size, -1)
    page_index = jnp.sum(
        jnp.where(page_owner_device[0][:, None] == sources[None, :], sources[:, None], 0), axis=0
    )
    page_spots = page_index[:, None] * page_size + jnp.arange(page_size, dtype=jnp.int32)[None, :]
    usable = (page_spots.reshape(1, -1) < cached_length[0]).astype(jnp.float32)

    query_vectors, block_keys, block_values = project(
        embeddings, norm_gain, query_key_value_weight, positions
    )
    target_shard = vocab_shard[:, 0]
    capacity = max(2, 2 * length // members)
    chosen = (target_shard[:, None] == sources[None, :]).astype(jnp.int32)
    earlier = (jnp.arange(length)[:, None] > jnp.arange(length)[None, :]).astype(jnp.int32)
    slot_rank = jnp.sum(jnp.dot(earlier, chosen) * chosen, axis=1)
    wanted = jnp.zeros((members, capacity), jnp.int32).at[target_shard, slot_rank].set(shard_row)
    asked = lax.all_to_all(wanted, "tok", split_axis=0, concat_axis=0, tiled=True)
    found_rows = jnp.take(embed_table, asked, axis=0)
    returned = lax.all_to_all(found_rows, "tok", split_axis=0, concat_axis=0, tiled=True)
    replacement = returned[target_shard, slot_rank]
    full_rows = lax.all_gather(replacement, "head", axis=1, tiled=True)
    replaced = jnp.where(accept[:, None] == 1, full_rows, embeddings)
    queries_two, keys_two, values_two = project(
        replaced, norm_gain, query_key_value_weight, positions
    )
    return attend_both(
        query_vectors, block_keys, block_values, queries_two, keys_two, values_two, pages, usable
    )


def solution(mesh):
    return jax.shard_map(
        body,
        mesh=mesh,
        in_specs=(
            P("tok", None),
            P(),
            P(None, "head"),
            P("tok", "head"),
            P("tok", None, None, "head"),
            P("tok", None),
            P("tok"),
            P("tok", None),
            P("tok"),
            P("tok"),
        ),
        out_specs=(P("tok", "head"), P("tok", "head")),
        check_vma=False,
    )
```

time: 243 us -> 181 us (0.74)
  matrix products: 47.7 us -> 11.8 us
  local copies, waits for them, and re-layouts: 42.5 us -> 16.8 us
  Pallas kernels: 0 us -> 17.8 us
  other arithmetic: 20.6 us -> 4.86 us
    dot_general x8 -> x0, matrix products: 35.5 us -> none  [the longest x2 17.1 us: attend(): jnp.einsum('gqbk,kgd->bgqd', weights_cache, page_values, preferred_elemen...]
    pallas_call x0 -> x1, Pallas kernels: none -> 17.8 us  [attend_both(): pl.pallas_call(attention_kernel, grid=(HEADS_PER_GROUP,), in_specs=[qspec...]
    reduce_sum x4 -> x0, other arithmetic: 17.1 us -> none  [attend(): totals = jnp.sum(exp_cache, axis=-1) + jnp.sum(exp_block, axis=-1)]
    slice x1 -> x2, local copies, waits for them, and re-layouts: 9.81 us -> 0.01 us  [project(): block_values = combined[:, :, HEADS_PER_GROUP + 1].astype(jnp.bfloat16)]
    unnamed x25 -> x23, local copies, waits for them, and re-layouts: 11.3 us -> 2.13 us
    reshape x1 -> x0, local copies, waits for them, and re-layouts: 6.92 us -> none  [body(): arrived = arrived.reshape(members * page_size, -1, 2, HEAD_SIZE)]
  transfers between devices with their start and end apart: 2 -> 2, of which waited for: 2 -> 2; matrix products, arithmetic and copies ran while one was open for 7% -> 10% of each run, Pallas kernels for 0% -> 0%
where the time goes in v1:
time: 181 us; the launch traced here: 180 us
  waiting for transfers between devices  72.8 us (40%)
  blocking collectives  34.2 us (19%)
  Pallas kernels  17.8 us (10%)
  local copies, waits for them, and re-layouts  16.8 us (9%)
  between operations  14.9 us (8%)
  matrix products  11.8 us (7%)
  starting transfers between devices  6.99 us (4%)
  other arithmetic  4.86 us (3%)
    all_to_all x1, waiting for transfers between devices, body(): lax.all_to_all(rotated_cache_pages, 'tok', split_axis=1, concat_axis=0, t...  47.8 us
    all_gather x1, waiting for transfers between devices, body(): full_rows = lax.all_gather(replacement, 'head', axis=1, tiled=True)  25 us
    all_to_all x1, blocking collectives, body(): lax.all_to_all(wanted, 'tok', split_axis=0, concat_axis=0, tiled=True)  19.1 us
    pallas_call x1, Pallas kernels, attend_both(): pl.pallas_call(attention_kernel, grid=(HEADS_PER_GROUP,), in_specs=[qspec...  17.8 us
    all_to_all x1, blocking collectives, body(): lax.all_to_all(found_rows, 'tok', split_axis=0, concat_axis=0, tiled=True)  15.1 us
    scatter x1, local copies, waits for them, and re-layouts, body(): jnp.zeros((members, capacity), jnp.int32).at[target_shard, slot_rank]  10.9 us
    dot_general x2, matrix products, project(): jnp.dot(normed, query_key_value_weight, preferred_element_type=jnp.float32)  10.8 us
    all_to_all x1, starting transfers between devices, body(): lax.all_to_all(rotated_cache_pages, 'tok', split_axis=1, concat_axis=0, t...  6.77 us
  transfers between devices with their start and end apart: 2, of which 2 were waited for; matrix products, arithmetic and copies ran while one was open for 10% of the time, Pallas kernels for 0%

profile of v1, /device:TPU:28, one launch (start us, length us, event | category | flops | bytes accessed | tf_op | source)
XLA Modules:
  0.0 180.1 jit_solution(1448388643950022316)
XLA Ops:
  7.2 0.0 copy-start
  7.2 1.0 fusion.6
  8.2 0.7 fusion.33
  8.8 10.9 %scatter_fusion = s32[32,8]{0,1:T(8,128)S(1)} fusion(s32[32,8]{0,1:T(8,128)S(1)} %broadcast_in_dim.32, s32[128]{0:T(128)S(1)} %get-tuple-element.4, s32[128]{0:T(128)} %param.18), kind=kCustom, calls=%fused_computation.2 | custom fusion | bytes 2560 | tf_op jit(solution)/shard_map/scatter | solution.py:163
  19.8 0.1 copy.54
  19.9 19.1 %all_to_all.29 = s32[32,1,8]{2,1,0:T(1,128)S(1)} all-to-all(s32[32,1,8]{2,1,0:T(1,128)S(1)} %copy.54), channel_id=1, replica_groups=mesh['tok'=32,'head'=8] {'tok'}, dimensions={0} | all-to-all | bytes 2048 | tf_op jit(solution)/shard_map/all_to_all | solution.py:164
  38.9 0.1 reshape.285
  39.0 0.1 copy.55
  39.1 0.1 copy.56
  39.2 0.0 copy-done
  39.2 1.2 gather_fusion
  40.4 0.1 bitcast_select_fusion
  40.5 15.1 %all_to_all.30 = bf16[32,8,512]{2,1,0:T(8,128)(2,1)S(1)} all-to-all(bf16[32,8,512]{2,1,0:T(8,128)(2,1)S(1)} %bitcast_select_fusion), channel_id=1, replica_groups=mesh['tok'=32,'head'=8] {'tok'}, dimensions={0} | all-to-all | bytes 524288 | tf_op jit(solution)/shard_map/all_to_all | solution.py:166
  55.6 0.0 copy-start.5
  55.6 0.0 copy-start.6
  55.6 0.0 copy-start.7
  55.6 6.8 %all-to-all-start.2 = ((bf16[1,32,256,256]{3,2,0,1:T(8,128)(2,1)}), bf16[1,32,256,256]{3,2,0,1:T(8,128)(2,1)}, u32[]{:S(2)}, u32[]{:S(2)}) async-start(bf16[1,32,256,256]{3,2,0,1:T(8,128)(2,1)} %bitcast.52), calls=%async_computation.2 | async-start | bytes 8388608 | tf_op jit(solution)/shard_map/all_to_all | solution.py:146
  62.4 0.0 copy-start.1
  62.4 0.2 all-gather.2.cloned.1.call-start
  62.6 1.9 %gather_fusion.1 = bf16[128,512]{1,0:T(8,128)(2,1)} fusion(bf16[32,8,512]{2,1,0:T(8,128)(2,1)S(1)} %all_to_all.30, s32[128]{0:T(128)S(1)} %bitcast.51), kind=kCustom, calls=%fused_computation.1 | custom fusion | bytes 263168 | tf_op jit(solution)/shard_map/gather | solution.py:167
  64.5 0.0 all-gather.2.cloned.1.call-update
  64.6 0.0 copy-done.5
  65.2 0.0 copy-done.6
  65.2 0.1 select_reduce_fusion
  65.3 0.1 convert_bitcast_fusion
  65.5 0.0 copy-done.7
  65.5 0.2 multiply_cosine_fusion.1
  65.7 25.0 %all-gather.2.cloned.1.call-done = bf16[128,4096]{1,0:T(8,128)(2,1)} async-done(((bf16[128,512]{1,0:T(8,128)(2,1)}), bf16[128,4096]{1,0:T(8,128)(2,1)}) %all-gather.2.cloned.1.call-update) | async-done | bytes 1048592 | tf_op jit(solution)/shard_map/all_gather | solution.py:168
  90.7 0.0 copy-done.1
  90.7 0.0 copy-start.3
  90.7 1.9 %fusion.3 = (f32[128]{0:T(128)S(1)}, f32[128]{0:T(128)S(1)}) fusion(bf16[128,4096]{1,0:T(8,128)(2,1)} %all-gather.2.cloned.1.call-done, bf16[128,4096]{1,0:T(8,128)(2,1)S(1)} %copy-done.1, pred[128]{0:T(512)(128)(4,1)S(1)} %broadcast_compare_fusion), kind=kLoop, calls=%fused_computation.10 | loop fusion | flops 3669760 | bytes 2098304 | tf_op jit(solution)/shard_map/reduce_sum | solution.py:39
  92.7 0.0 copy-done.3
  92.7 5.4 %fusion.7 = f32[128,768]{0,1:T(8,128)S(1)} fusion(bf16[4096,768]{1,0:T(8,128)(2,1)} %param.12, f32[128]{0:T(128)S(1)} %get-tuple-element.24, f32[4096]{0:T(1024)S(1)} %convert_element_type.74, bf16[128,4096]{1,0:T(8,128)(2,1)S(1)} %copy-done.3, bf16[128,4096]{1,0:T(8,128)(2,1)S(1)} %copy-done.1, pred[128]{0:T(512)(128)(4,1)S(1)} %broadcast_compare_fusion), kind=kOutput, calls=%fused_computation.15 | convolution fusion | flops 807927808 | bytes 8798848 | tf_op jit(solution)/shard_map/dot_general | solution.py:41
  98.1 0.0 copy-start.4
  98.2 0.7 copy-done.4
  98.9 0.1 copy.73
  99.0 0.1 copy.74
  99.1 5.4 %fusion.9 = f32[128,768]{0,1:T(8,128)S(1)} fusion(bf16[4096,768]{1,0:T(8,128)(2,1)} %param.12, bf16[128,4096]{1,0:T(8,128)(2,1)S(1)} %copy-done.1, f32[4096]{0:T(1024)S(1)} %convert_element_type.74, f32[128]{0:T(128)S(1)} %get-tuple-element.25), kind=kOutput, calls=%fused_computation.16 | convolution fusion | flops 807403520 | bytes 7750144 | tf_op jit(solution)/shard_map/dot_general | solution.py:41
  104.5 0.0 copy-start.2
  104.5 0.7 copy-done.2
  105.2 0.1 copy.70
  105.3 0.1 copy.71
  105.4 1.2 subtract_convert_fusion
  106.6 0.1 copy.67.q2_ref
  106.8 0.1 copy.66.q1_ref
  106.9 0.1 copy.75
  107.0 0.1 copy.72
  107.1 0.4 fusion.28
  107.5 0.1 maximum_bitcast_fusion.1.kb2_ref
  107.6 0.1 maximum_bitcast_fusion.kb1_ref
  107.7 47.8 %all-to-all-done.2 = bf16[1,32,256,256]{3,2,0,1:T(8,128)(2,1)} async-done(((bf16[1,32,256,256]{3,2,0,1:T(8,128)(2,1)}), bf16[1,32,256,256]{3,2,0,1:T(8,128)(2,1)}, u32[]{:S(2)}, u32[]{:S(2)}) %all-to-all-start.2) | async-done | bytes 4194336 | tf_op jit(solution)/shard_map/all_to_all | solution.py:146
  155.4 17.8 %shard_map.113 = (bf16[128,512]{1,0:T(8,128)(2,1)}, bf16[128,512]{1,0:T(8,128)(2,1)}) custom-call(bf16[128,512]{1,0:T(8,128)(2,1)S(1)} %copy.66.q1_ref, bf16[128,512]{1,0:T(8,128)(2,1)S(1)} %copy.67.q2_ref, bf16[128,128]{1,0:T(8,128)(2,1)S(1)} %maximum_bitcast_fusion.kb1_ref, bf16[128,128]{1,0:T(8,128)(2,1)S(1)} %bitcast.49, ...), custom_call_target="tpu_custom_call" | custom-call | tf_op jit(solution)/shard_map/pallas_call | solution.py:107
  (17 shorter events, 0.1 us)
Async XLA Ops:
  7.2 32.0 %copy-start = (bf16[2048,512]{1,0:T(8,128)(2,1)S(1)}, bf16[2048,512]{1,0:T(8,128)(2,1)}, u32[]{:S(2)}) copy-start(bf16[2048,512]{1,0:T(8,128)(2,1)} %param.13) | copy-start | bytes 6291460
  55.6 9.0 %copy-start.5 = (bf16[4096]{0:T(1024)(128)(2,1)S(1)}, bf16[4096]{0:T(1024)(128)(2,1)}, u32[]{:S(2)}) copy-start(bf16[4096]{0:T(1024)(128)(2,1)} %param.11) | copy-start | bytes 24580
  55.6 9.7 %copy-start.6 = (s32[1,32]{1,0:T(1,128)S(1)}, s32[1,32]{1,0:T(1,128)}, u32[]{:S(2)}) copy-start(s32[1,32]{1,0:T(1,128)} %param.15) | copy-start | bytes 388
  55.6 9.9 %copy-start.7 = (s32[128]{0:T(128)S(1)}, s32[128]{0:T(128)}, u32[]{:S(2)}) copy-start(s32[128]{0:T(128)} %param.19) | copy-start | bytes 1540
  55.6 99.9 %all-to-all-start.2 = ((bf16[1,32,256,256]{3,2,0,1:T(8,128)(2,1)}), bf16[1,32,256,256]{3,2,0,1:T(8,128)(2,1)}, u32[]{:S(2)}, u32[]{:S(2)}) async-start(bf16[1,32,256,256]{3,2,0,1:T(8,128)(2,1)} %bitcast.52), calls=%async_computation.2 | async-start | bytes 8388608 | tf_op jit(solution)/shard_map/all_to_all | solution.py:146
  62.4 28.4 %copy-start.1 = (bf16[128,4096]{1,0:T(8,128)(2,1)S(1)}, bf16[128,4096]{1,0:T(8,128)(2,1)}, u32[]{:S(2)}) copy-start(bf16[128,4096]{1,0:T(8,128)(2,1)} %param.10) | copy-start | bytes 3145732
  62.4 28.4 %all-gather.2.cloned.1.call-start = ((), (), s32[]{:S(2)}) async-start(), calls=%async_computation.3 | async-start | bytes 1179648 | tf_op jit(solution)/shard_map/all_gather | solution.py:168
  90.7 2.0 %copy-start.3 = (bf16[128,4096]{1,0:T(8,128)(2,1)S(1)}, bf16[128,4096]{1,0:T(8,128)(2,1)}, u32[]{:S(2)}) copy-start(bf16[128,4096]{1,0:T(8,128)(2,1)} %all-gather.2.cloned.1.call-done) | copy-start | bytes 3145732
  98.1 0.7 copy-start.4
  104.5 0.8 copy-start.2
Sparse Core Ops, SparseCore 0:
  65.6 25.0 all-gather.1

commit v2 on v1

--- a/solution.py
+++ b/solution.py
@@ -160,7 +160,11 @@
     chosen = (target_shard[:, None] == sources[None, :]).astype(jnp.int32)
     earlier = (jnp.arange(length)[:, None] > jnp.arange(length)[None, :]).astype(jnp.int32)
     slot_rank = jnp.sum(jnp.dot(earlier, chosen) * chosen, axis=1)
-    wanted = jnp.zeros((members, capacity), jnp.int32).at[target_shard, slot_rank].set(shard_row)
+    slot_of = target_shard * capacity + slot_rank
+    slots = jnp.arange(members * capacity, dtype=jnp.int32)
+    wanted = jnp.sum(
+        jnp.where(slot_of[:, None] == slots[None, :], shard_row[:, None], 0), axis=0
+    ).reshape(members, capacity)
     asked = lax.all_to_all(wanted, "tok", split_axis=0, concat_axis=0, tiled=True)
     found_rows = jnp.take(embed_table, asked, axis=0)
     returned = lax.all_to_all(found_rows, "tok", split_axis=0, concat_axis=0, tiled=True)

time: 181 us -> 170 us (0.939)
  local copies, waits for them, and re-layouts: 16.8 us -> 5.67 us
    scatter x1 -> x0, local copies, waits for them, and re-layouts: 10.9 us -> none  [body(): jnp.zeros((members, capacity), jnp.int32).at[target_shard, slot_rank]]
where the time goes in v2:
time: 170 us
  waiting for transfers between devices  72.8 us (43%)
  blocking collectives  34.2 us (20%)
  Pallas kernels  17.8 us (10%)
  between operations  14.9 us (9%)
  matrix products  11.8 us (7%)
  starting transfers between devices  6.99 us (4%)
  local copies, waits for them, and re-layouts  5.67 us (3%)
  other arithmetic  5.62 us (3%)
    all_to_all x1, waiting for transfers between devices, body(): lax.all_to_all(rotated_cache_pages, 'tok', split_axis=1, concat_axis=0, t...  47.7 us
    all_gather x1, waiting for transfers between devices, body(): full_rows = lax.all_gather(replacement, 'head', axis=1, tiled=True)  25 us
    all_to_all x1, blocking collectives, body(): lax.all_to_all(wanted, 'tok', split_axis=0, concat_axis=0, tiled=True)  19.1 us
    pallas_call x1, Pallas kernels, attend_both(): pl.pallas_call(attention_kernel, grid=(HEADS_PER_GROUP,), in_specs=[qspec...  17.8 us
    all_to_all x1, blocking collectives, body(): lax.all_to_all(found_rows, 'tok', split_axis=0, concat_axis=0, tiled=True)  15.1 us
    dot_general x2, matrix products, project(): jnp.dot(normed, query_key_value_weight, preferred_element_type=jnp.float32)  10.8 us
    all_to_all x1, starting transfers between devices, body(): lax.all_to_all(rotated_cache_pages, 'tok', split_axis=1, concat_axis=0, t...  6.77 us
  transfers between devices with their start and end apart: 2, of which 2 were waited for; matrix products, arithmetic and copies ran while one was open for 10% of the time, Pallas kernels for 0%

profile of v2, /device:TPU:28, one launch (start us, length us, event | category | flops | bytes accessed | tf_op | source)
XLA Modules:
  0.0 169.8 jit_solution(2289135401649707546)
XLA Ops:
  7.2 0.0 copy-start
  7.2 1.0 fusion.6
  8.2 0.7 fusion.38
  8.8 0.8 select_reduce_fusion
  9.6 0.1 all_to_all.20
  9.7 19.1 %all_to_all.29 = s32[32,1,8]{2,1,0:T(1,128)S(1)} all-to-all(s32[32,1,8]{2,1,0:T(1,128)S(1)} %bitcast.59), channel_id=1, replica_groups=mesh['tok'=32,'head'=8] {'tok'}, dimensions={0} | all-to-all | bytes 2048 | tf_op jit(solution)/shard_map/all_to_all | solution.py:168
  28.8 0.1 reshape.289
  28.9 0.0 copy-done
  28.9 1.2 gather_fusion
  30.0 0.1 bitcast_select_fusion
  30.2 15.1 %all_to_all.30 = bf16[32,8,512]{2,1,0:T(8,128)(2,1)S(1)} all-to-all(bf16[32,8,512]{2,1,0:T(8,128)(2,1)S(1)} %bitcast_select_fusion), channel_id=1, replica_groups=mesh['tok'=32,'head'=8] {'tok'}, dimensions={0} | all-to-all | bytes 524288 | tf_op jit(solution)/shard_map/all_to_all | solution.py:170
  45.3 0.0 copy-start.5
  45.3 0.0 copy-start.6
  45.3 0.0 copy-start.7
  45.3 6.8 %all-to-all-start.2 = ((bf16[1,32,256,256]{3,2,0,1:T(8,128)(2,1)}), bf16[1,32,256,256]{3,2,0,1:T(8,128)(2,1)}, u32[]{:S(2)}, u32[]{:S(2)}) async-start(bf16[1,32,256,256]{3,2,0,1:T(8,128)(2,1)} %bitcast.48), calls=%async_computation.2 | async-start | bytes 8388608 | tf_op jit(solution)/shard_map/all_to_all | solution.py:146
  52.0 0.0 copy-start.1
  52.0 0.2 all-gather.2.cloned.1.call-start
  52.3 1.9 %gather_fusion.1 = bf16[128,512]{1,0:T(8,128)(2,1)} fusion(bf16[32,8,512]{2,1,0:T(8,128)(2,1)S(1)} %all_to_all.30, s32[128]{0:T(128)S(1)} %get-tuple-element.22), kind=kCustom, calls=%fused_computation.1 | custom fusion | bytes 263168 | tf_op jit(solution)/shard_map/gather | solution.py:171
  54.2 0.0 all-gather.2.cloned.1.call-update
  54.2 0.0 copy-done.5
  54.9 0.0 copy-done.6
  54.9 0.1 select_reduce_fusion.1
  55.0 0.1 convert_bitcast_fusion
  55.2 0.0 copy-done.7
  55.2 0.2 multiply_cosine_fusion.1
  55.4 25.0 %all-gather.2.cloned.1.call-done = bf16[128,4096]{1,0:T(8,128)(2,1)} async-done(((bf16[128,512]{1,0:T(8,128)(2,1)}), bf16[128,4096]{1,0:T(8,128)(2,1)}) %all-gather.2.cloned.1.call-update) | async-done | bytes 1048592 | tf_op jit(solution)/shard_map/all_gather | solution.py:172
  80.4 0.0 copy-done.1
  80.4 0.0 copy-start.3
  80.4 1.9 %fusion.3 = (f32[128]{0:T(128)S(1)}, f32[128]{0:T(128)S(1)}) fusion(bf16[128,4096]{1,0:T(8,128)(2,1)} %all-gather.2.cloned.1.call-done, bf16[128,4096]{1,0:T(8,128)(2,1)S(1)} %copy-done.1, pred[128]{0:T(512)(128)(4,1)S(1)} %broadcast_compare_fusion), kind=kLoop, calls=%fused_computation.9 | loop fusion | flops 3669760 | bytes 2098304 | tf_op jit(solution)/shard_map/reduce_sum | solution.py:39
  82.4 0.0 copy-done.3
  82.4 5.4 %fusion.7 = f32[128,768]{0,1:T(8,128)S(1)} fusion(bf16[4096,768]{1,0:T(8,128)(2,1)} %param.12, f32[128]{0:T(128)S(1)} %get-tuple-element.24, f32[4096]{0:T(1024)S(1)} %convert_element_type.74, bf16[128,4096]{1,0:T(8,128)(2,1)S(1)} %copy-done.3, bf16[128,4096]{1,0:T(8,128)(2,1)S(1)} %copy-done.1, pred[128]{0:T(512)(128)(4,1)S(1)} %broadcast_compare_fusion), kind=kOutput, calls=%fused_computation.14 | convolution fusion | flops 807927808 | bytes 8798848 | tf_op jit(solution)/shard_map/dot_general | solution.py:41
  87.8 0.0 copy-start.4
  87.8 0.7 copy-done.4
  88.6 0.1 copy.64
  88.7 0.1 copy.65
  88.8 5.4 %fusion.9 = f32[128,768]{0,1:T(8,128)S(1)} fusion(bf16[4096,768]{1,0:T(8,128)(2,1)} %param.12, bf16[128,4096]{1,0:T(8,128)(2,1)S(1)} %copy-done.1, f32[4096]{0:T(1024)S(1)} %convert_element_type.74, f32[128]{0:T(128)S(1)} %get-tuple-element.25), kind=kOutput, calls=%fused_computation.15 | convolution fusion | flops 807403520 | bytes 7750144 | tf_op jit(solution)/shard_map/dot_general | solution.py:41
  94.2 0.0 copy-start.2
  94.2 0.7 copy-done.2
  94.9 0.1 copy.61
  95.0 0.1 copy.62
  95.1 1.2 subtract_convert_fusion
  96.3 0.1 copy.58.q2_ref
  96.5 0.1 copy.57.q1_ref
  96.6 0.1 copy.66
  96.7 0.1 copy.63
  96.8 0.4 fusion.28
  97.2 0.1 maximum_bitcast_fusion.1.kb2_ref
  97.3 0.1 maximum_bitcast_fusion.kb1_ref
  97.4 47.7 %all-to-all-done.2 = bf16[1,32,256,256]{3,2,0,1:T(8,128)(2,1)} async-done(((bf16[1,32,256,256]{3,2,0,1:T(8,128)(2,1)}), bf16[1,32,256,256]{3,2,0,1:T(8,128)(2,1)}, u32[]{:S(2)}, u32[]{:S(2)}) %all-to-all-start.2) | async-done | bytes 4194336 | tf_op jit(solution)/shard_map/all_to_all | solution.py:146
  145.1 17.8 %shard_map.113 = (bf16[128,512]{1,0:T(8,128)(2,1)}, bf16[128,512]{1,0:T(8,128)(2,1)}) custom-call(bf16[128,512]{1,0:T(8,128)(2,1)S(1)} %copy.57.q1_ref, bf16[128,512]{1,0:T(8,128)(2,1)S(1)} %copy.58.q2_ref, bf16[128,128]{1,0:T(8,128)(2,1)S(1)} %maximum_bitcast_fusion.kb1_ref, bf16[128,128]{1,0:T(8,128)(2,1)S(1)} %bitcast.47, ...), custom_call_target="tpu_custom_call" | custom-call | tf_op jit(solution)/shard_map/pallas_call | solution.py:107
  (16 shorter events, 0.1 us)
Async XLA Ops:
  7.2 21.7 %copy-start = (bf16[2048,512]{1,0:T(8,128)(2,1)S(1)}, bf16[2048,512]{1,0:T(8,128)(2,1)}, u32[]{:S(2)}) copy-start(bf16[2048,512]{1,0:T(8,128)(2,1)} %param.13) | copy-start | bytes 6291460
  45.3 9.0 %copy-start.5 = (bf16[4096]{0:T(1024)(128)(2,1)S(1)}, bf16[4096]{0:T(1024)(128)(2,1)}, u32[]{:S(2)}) copy-start(bf16[4096]{0:T(1024)(128)(2,1)} %param.11) | copy-start | bytes 24580
  45.3 9.7 %copy-start.6 = (s32[1,32]{1,0:T(1,128)S(1)}, s32[1,32]{1,0:T(1,128)}, u32[]{:S(2)}) copy-start(s32[1,32]{1,0:T(1,128)} %param.15) | copy-start | bytes 388
  45.3 9.9 %copy-start.7 = (s32[128]{0:T(128)S(1)}, s32[128]{0:T(128)}, u32[]{:S(2)}) copy-start(s32[128]{0:T(128)} %param.19) | copy-start | bytes 1540
  45.3 99.9 %all-to-all-start.2 = ((bf16[1,32,256,256]{3,2,0,1:T(8,128)(2,1)}), bf16[1,32,256,256]{3,2,0,1:T(8,128)(2,1)}, u32[]{:S(2)}, u32[]{:S(2)}) async-start(bf16[1,32,256,256]{3,2,0,1:T(8,128)(2,1)} %bitcast.48), calls=%async_computation.2 | async-start | bytes 8388608 | tf_op jit(solution)/shard_map/all_to_all | solution.py:146
  52.0 28.4 %copy-start.1 = (bf16[128,4096]{1,0:T(8,128)(2,1)S(1)}, bf16[128,4096]{1,0:T(8,128)(2,1)}, u32[]{:S(2)}) copy-start(bf16[128,4096]{1,0:T(8,128)(2,1)} %param.10) | copy-start | bytes 3145732
  52.0 28.4 %all-gather.2.cloned.1.call-start = ((), (), s32[]{:S(2)}) async-start(), calls=%async_computation.3 | async-start | bytes 1179648 | tf_op jit(solution)/shard_map/all_gather | solution.py:172
  80.4 2.0 %copy-start.3 = (bf16[128,4096]{1,0:T(8,128)(2,1)S(1)}, bf16[128,4096]{1,0:T(8,128)(2,1)}, u32[]{:S(2)}) copy-start(bf16[128,4096]{1,0:T(8,128)(2,1)} %all-gather.2.cloned.1.call-done) | copy-start | bytes 3145732
  87.8 0.8 copy-start.4
  94.2 0.8 copy-start.2
Sparse Core Ops, SparseCore 0:
  55.3 25.0 all-gather.1

commit v3 on v1

--- a/solution.py
+++ b/solution.py
@@ -156,17 +156,36 @@
         embeddings, norm_gain, query_key_value_weight, positions
     )
     target_shard = vocab_shard[:, 0]
-    capacity = max(2, 2 * length // members)
-    chosen = (target_shard[:, None] == sources[None, :]).astype(jnp.int32)
-    earlier = (jnp.arange(length)[:, None] > jnp.arange(length)[None, :]).astype(jnp.int32)
-    slot_rank = jnp.sum(jnp.dot(earlier, chosen) * chosen, axis=1)
-    wanted = jnp.zeros((members, capacity), jnp.int32).at[target_shard, slot_rank].set(shard_row)
-    asked = lax.all_to_all(wanted, "tok", split_axis=0, concat_axis=0, tiled=True)
-    found_rows = jnp.take(embed_table, asked, axis=0)
-    returned = lax.all_to_all(found_rows, "tok", split_axis=0, concat_axis=0, tiled=True)
-    replacement = returned[target_shard, slot_rank]
-    full_rows = lax.all_gather(replacement, "head", axis=1, tiled=True)
-    replaced = jnp.where(accept[:, None] == 1, full_rows, embeddings)
+    most = members
+    taken = accept == 1
+    order = jnp.cumsum(taken.astype(jnp.int32)) - 1
+    slots = jnp.arange(most, dtype=jnp.int32)
+    hit = taken[:, None] & (order[:, None] == slots[None, :])
+    filled = jnp.any(hit, axis=0)
+    req_shard = jnp.where(filled, jnp.sum(jnp.where(hit, target_shard[:, None], 0), axis=0), -1)
+    req_row = jnp.sum(jnp.where(hit, shard_row[:, None], 0), axis=0)
+    request = jnp.stack([req_shard, req_row]).astype(jnp.float32)
+    request = jnp.pad(request, ((0, 0), (0, 512 - most)))
+    me = lax.axis_index("tok")
+    placed = jnp.where((sources == me)[:, None, None], request[None], jnp.zeros((), request.dtype))
+    every_request = lax.psum(placed, "tok")
+    from_here = every_request[:, 0, :most].astype(jnp.int32) == me
+    rows_here = jnp.clip(every_request[:, 1, :most].astype(jnp.int32), 0, embed_table.shape[0] - 1)
+    looked = jnp.take(embed_table, rows_here.reshape(-1), axis=0).reshape(
+        members, most, embed_table.shape[1]
+    )
+    looked = jnp.where(from_here[:, :, None], looked, jnp.zeros((), looked.dtype))
+    mine = lax.psum_scatter(looked, "tok", scatter_dimension=0, tiled=True)[0]
+    group = lax.axis_index("head")
+    groups = lax.axis_size("head")
+    spread = jnp.where(
+        (jnp.arange(groups) == group)[None, :, None],
+        mine[:, None, :],
+        jnp.zeros((), mine.dtype),
+    )
+    full_rows = lax.psum(spread, "head").reshape(mine.shape[0], -1)
+    picked = jnp.take(full_rows, jnp.clip(order, 0, most - 1), axis=0)
+    replaced = jnp.where(taken[:, None], picked, embeddings)
     queries_two, keys_two, values_two = project(
         replaced, norm_gain, query_key_value_weight, positions
     )

time: 181 us -> 512 us (2.83)
  waiting for transfers between devices: 72.8 us -> 432 us
  blocking collectives: 34.2 us -> 0 us
  local copies, waits for them, and re-layouts: 16.8 us -> 10.5 us
  other arithmetic: 4.86 us -> 11 us
    psum x0 -> x2, waiting for transfers between devices: none -> 218 us  [the longest x1 155 us: body(): every_request = lax.psum(placed, 'tok')]
    reduce_scatter x0 -> x1, waiting for transfers between devices: none -> 214 us  [body(): mine = lax.psum_scatter(looked, 'tok', scatter_dimension=0, tiled=True)[0]]
    all_to_all x1, waiting for transfers between devices: 47.8 us -> 0.01 us  [body(): lax.all_to_all(rotated_cache_pages, 'tok', split_axis=1, concat_axis=0, t...]
    all_to_all x2 -> x0, blocking collectives: 34.2 us -> none  [the longest x1 19.1 us: body(): lax.all_to_all(wanted, 'tok', split_axis=0, concat_axis=0, tiled=True)]
    all_gather x1 -> x0, waiting for transfers between devices: 25 us -> none  [body(): full_rows = lax.all_gather(replacement, 'head', axis=1, tiled=True)]
    scatter x1 -> x0, local copies, waits for them, and re-layouts: 10.9 us -> none  [body(): jnp.zeros((members, capacity), jnp.int32).at[target_shard, slot_rank]]
  transfers between devices with their start and end apart: 2 -> 4, of which waited for: 2 -> 3; matrix products, arithmetic and copies ran while one was open for 10% -> 6% of each run, Pallas kernels for 0% -> 0%
where the time goes in v3:
time: 512 us; the launch traced here: 509 us
  waiting for transfers between devices  432 us (84%)
  Pallas kernels  18 us (4%)
  between operations  14.8 us (3%)
  starting transfers between devices  11.9 us (2%)
  other arithmetic  11 us (2%)
  matrix products  10.9 us (2%)
  local copies, waits for them, and re-layouts  10.5 us (2%)
    reduce_scatter x1, waiting for transfers between devices, body(): mine = lax.psum_scatter(looked, 'tok', scatter_dimension=0, tiled=True)[0]  214 us
    psum x1, waiting for transfers between devices, body(): every_request = lax.psum(placed, 'tok')  155 us
    psum x1, waiting for transfers between devices, body(): full_rows = lax.psum(spread, 'head').reshape(mine.shape[0], -1)  62.9 us
    pallas_call x1, Pallas kernels, attend_both(): pl.pallas_call(attention_kernel, grid=(HEADS_PER_GROUP,), in_specs=[qspec...  18 us
    all_to_all x1, starting transfers between devices, body(): lax.all_to_all(rotated_cache_pages, 'tok', split_axis=1, concat_axis=0, t...  11.8 us
    dot_general x2, matrix products, project(): jnp.dot(normed, query_key_value_weight, preferred_element_type=jnp.float32)  10.9 us
  transfers between devices with their start and end apart: 4, of which 3 were waited for; matrix products, arithmetic and copies ran while one was open for 6% of the time, Pallas kernels for 0%

profile of v3, /device:TPU:28, one launch (start us, length us, event | category | flops | bytes accessed | tf_op | source)
XLA Modules:
  0.0 509.0 jit_solution(16252518622337274740)
XLA Ops:
  7.2 0.0 copy-start
  7.2 0.0 copy-start.8
  7.2 0.0 copy-start.6
  7.2 0.0 copy-start.7
  7.2 11.8 %all-to-all-start = ((bf16[1,32,256,256]{3,2,0,1:T(8,128)(2,1)}), bf16[1,32,256,256]{3,2,0,1:T(8,128)(2,1)}, u32[]{:S(2)}, u32[]{:S(2)}) async-start(bf16[1,32,256,256]{3,2,0,1:T(8,128)(2,1)} %bitcast.49), calls=%async_computation.1 | async-start | bytes 8388608 | tf_op jit(solution)/shard_map/all_to_all | solution.py:146
  19.0 0.0 all-reduce.4.cloned.1.call-start
  19.1 0.0 copy-done.8
  19.1 0.1 copy.49
  19.2 0.2 reduce-window.4
  19.4 0.1 fusion.30
  19.5 0.1 fusion.34
  19.6 0.0 copy-done.6
  19.6 0.0 copy-done.7
  19.6 0.1 select_reduce_fusion.2
  19.8 0.7 broadcast_select_fusion.1
  20.5 0.0 all-reduce.4.cloned.1.call-update
  20.5 0.0 reduce-scatter.2.cloned.1.call-start
  20.6 155.1 %all-reduce.4.cloned.1.call-done = f32[32,2,512]{2,0,1:T(8,128)} async-done(((f32[32,2,512]{2,0,1:T(8,128)}), f32[32,2,512]{2,0,1:T(8,128)}) %all-reduce.4.cloned.1.call-update) | async-done | bytes 131088 | tf_op jit(solution)/shard_map/psum | solution.py:171
  175.6 0.7 fusion.31
  176.4 0.1 min.32
  176.5 0.0 copy-done
  176.5 4.0 gather_fusion
  180.4 0.0 copy-start.9
  180.5 0.7 fusion.35
  181.2 0.7 compare_and_fusion
  181.9 0.0 copy-start.5
  181.9 1.3 select_select_fusion.1
  183.2 0.0 reduce-scatter.2.cloned.1.call-update
  183.2 0.0 all-reduce.6.cloned.1.call-start
  184.0 0.0 copy-done.9
  184.0 0.1 select_reduce_fusion
  184.1 0.1 convert_bitcast_fusion
  184.1 0.2 multiply_cosine_fusion.1
  184.3 213.9 %reduce-scatter.2.cloned.1.call-done = bf16[1,32,512]{2,1,0:T(8,128)(2,1)} async-done(((bf16[32,32,512]{2,1,0:T(8,128)(2,1)}), bf16[1,32,512]{2,1,0:T(8,128)(2,1)}) %reduce-scatter.2.cloned.1.call-update) | async-done | bytes 32784 | tf_op jit(solution)/shard_map/reduce_scatter | solution.py:178
  398.3 0.8 broadcast_select_fusion
  399.1 0.8 copy.69
  399.9 0.0 all-reduce.6.cloned.1.call-update
  399.9 0.0 copy-done.5
  400.0 62.9 %all-reduce.6.cloned.1.call-done = bf16[32,4096]{1,0:T(8,128)(2,1)} async-done(((bf16[32,4096]{1,0:T(8,128)(2,1)}), bf16[32,4096]{1,0:T(8,128)(2,1)}) %all-reduce.6.cloned.1.call-update) | async-done | bytes 262160 | tf_op jit(solution)/shard_map/psum | solution.py:186
  462.9 3.2 gather_fusion.1
  466.1 0.0 copy-start.1
  466.1 3.3 fusion.3
  469.4 0.0 copy-done.1
  469.4 0.0 copy-start.2
  469.4 5.5 %fusion.8 = f32[128,768]{0,1:T(8,128)S(1)} fusion(bf16[4096,768]{1,0:T(8,128)(2,1)} %param.12, bf16[128,4096]{1,0:T(8,128)(2,1)S(1)} %copy-done.1, f32[4096]{0:T(1024)S(1)} %convert_element_type.102, f32[128]{0:T(128)S(1)} %get-tuple-element.30), kind=kOutput, calls=%fused_computation.13 | convolution fusion | flops 807403520 | bytes 7750144 | tf_op jit(solution)/shard_map/dot_general | solution.py:41
  474.9 0.0 copy-start.3
  474.9 0.7 copy-done.3
  475.6 0.1 copy.63
  475.7 0.1 copy.64
  475.8 0.0 copy-done.2
  475.9 5.4 %fusion.6 = f32[128,768]{0,1:T(8,128)S(1)} fusion(bf16[4096,768]{1,0:T(8,128)(2,1)} %param.12, bf16[128,4096]{1,0:T(8,128)(2,1)S(1)} %copy-done.2, f32[128]{0:T(128)S(1)} %get-tuple-element.29, f32[4096]{0:T(1024)S(1)} %convert_element_type.102), kind=kOutput, calls=%fused_computation.12 | convolution fusion | flops 807403520 | bytes 7750144 | tf_op jit(solution)/shard_map/dot_general | solution.py:41
  481.3 0.7 copy-done.4
  482.0 0.1 copy.66
  482.1 0.1 copy.67
  482.2 1.2 subtract_convert_fusion
  483.4 0.1 copy.60.q2_ref
  483.5 0.1 copy.59.q1_ref
  483.7 0.1 copy.68
  483.8 0.1 copy.65
  483.9 0.4 fusion.27
  484.3 0.1 maximum_bitcast_fusion.1.kb2_ref
  484.3 0.1 maximum_bitcast_fusion.kb1_ref
  484.4 0.0 all-to-all-done
  484.4 18.0 %shard_map.113 = (bf16[128,512]{1,0:T(8,128)(2,1)}, bf16[128,512]{1,0:T(8,128)(2,1)}) custom-call(bf16[128,512]{1,0:T(8,128)(2,1)S(1)} %copy.59.q1_ref, bf16[128,512]{1,0:T(8,128)(2,1)S(1)} %copy.60.q2_ref, bf16[128,128]{1,0:T(8,128)(2,1)S(1)} %maximum_bitcast_fusion.kb1_ref, bf16[128,128]{1,0:T(8,128)(2,1)S(1)} %bitcast.47, ...), custom_call_target="tpu_custom_call" | custom-call | tf_op jit(solution)/shard_map/pallas_call | solution.py:107
  (23 shorter events, 0.2 us)
Async XLA Ops:
  7.2 169.3 %copy-start = (bf16[2048,512]{1,0:T(8,128)(2,1)S(1)}, bf16[2048,512]{1,0:T(8,128)(2,1)}, u32[]{:S(2)}) copy-start(bf16[2048,512]{1,0:T(8,128)(2,1)} %param.13) | copy-start | bytes 6291460
  7.2 11.9 %copy-start.8 = (s32[128]{0:T(128)S(1)}, s32[128]{0:T(128)}, u32[]{:S(2)}) copy-start(s32[128]{0:T(128)} %param.19) | copy-start | bytes 1540
  7.2 12.4 %copy-start.6 = (s32[128,1]{0,1:T(1,128)S(1)}, s32[128,1]{0,1:T(1,128)}, u32[]{:S(2)}) copy-start(s32[128,1]{0,1:T(1,128)} %param.17) | copy-start | bytes 1540
  7.2 12.4 %copy-start.7 = (s32[128]{0:T(128)S(1)}, s32[128]{0:T(128)}, u32[]{:S(2)}) copy-start(s32[128]{0:T(128)} %param.18) | copy-start | bytes 1540
  7.2 477.2 %all-to-all-start = ((bf16[1,32,256,256]{3,2,0,1:T(8,128)(2,1)}), bf16[1,32,256,256]{3,2,0,1:T(8,128)(2,1)}, u32[]{:S(2)}, u32[]{:S(2)}) async-start(bf16[1,32,256,256]{3,2,0,1:T(8,128)(2,1)} %bitcast.49), calls=%async_computation.1 | async-start | bytes 8388608 | tf_op jit(solution)/shard_map/all_to_all | solution.py:146
  19.0 156.6 %all-reduce.4.cloned.1.call-start = ((), (), s32[]{:S(2)}) async-start(), calls=%async_computation.2 | async-start | bytes 262144 | tf_op jit(solution)/shard_map/psum | solution.py:171
  20.5 377.7 %reduce-scatter.2.cloned.1.call-start = ((), (), s32[]{:S(2)}) async-start(), calls=%async_computation.3 | async-start | bytes 1081344 | tf_op jit(solution)/shard_map/reduce_scatter | solution.py:178
  180.4 3.5 copy-start.9
  181.9 218.0 %copy-start.5 = (bf16[4096]{0:T(1024)(128)(2,1)S(1)}, bf16[4096]{0:T(1024)(128)(2,1)}, u32[]{:S(2)}) copy-start(bf16[4096]{0:T(1024)(128)(2,1)} %param.11) | copy-start | bytes 24580
  183.2 279.7 %all-reduce.6.cloned.1.call-start = ((), (), s32[]{:S(2)}) async-start(), calls=%async_computation.4 | async-start | bytes 524288 | tf_op jit(solution)/shard_map/psum | solution.py:186
  466.1 3.3 copy-start.1
  469.4 6.5 %copy-start.2 = (bf16[128,4096]{1,0:T(8,128)(2,1)S(1)}, bf16[128,4096]{1,0:T(8,128)(2,1)}, u32[]{:S(2)}) copy-start(bf16[128,4096]{1,0:T(8,128)(2,1)} %get-tuple-element.7) | copy-start | bytes 3145732
  474.9 0.7 copy-start.3
  481.2 0.8 copy-start.4
Sparse Core Ops, SparseCore 0:
  23.8 151.7 all-reduce.3
  183.3 214.8 reduce-scatter.1
  400.6 62.2 all-reduce.5

commit v4 on v2

v4 whole, which is shorter than its diff:
```python
import math

import jax
import jax.numpy as jnp
from jax import lax
from jax.experimental import pallas as pl
from jax.experimental.pallas import tpu as pltpu
from jax.sharding import PartitionSpec as P


QUERY_HEADS = 32
KEY_VALUE_HEADS = 8
HEAD_SIZE = 128
HEADS_PER_GROUP = QUERY_HEADS // KEY_VALUE_HEADS


THETA = 500000.0
PAGE_ROWS = 256
ID_ROWS = 8
ID_SPLIT = 64


def angles(positions):
    steps_half = jnp.arange(HEAD_SIZE // 2, dtype=jnp.float32)
    frequency = THETA ** (-(steps_half * 2.0) / HEAD_SIZE)
    return positions.astype(jnp.float32)[:, None] * frequency[None, :]


def rotate(vectors, turning):
    half_width = vectors.shape[-1] // 2
    former = vectors[..., :half_width]
    latter = vectors[..., half_width:]
    cosine = jnp.cos(turning)
    sine_of = jnp.sin(turning)
    return jnp.concatenate(
        [former * cosine - latter * sine_of, latter * cosine + former * sine_of], axis=-1
    )


def project(inputs, norm_gain, query_key_value_weight, positions, turning=None):
    widened = inputs.astype(jnp.float32)
    inverse = lax.rsqrt(jnp.mean(widened * widened, axis=-1, keepdims=True) + 1e-05)
    normed = (widened * inverse * norm_gain.astype(jnp.float32)).astype(jnp.bfloat16)
    combined = jnp.dot(normed, query_key_value_weight, preferred_element_type=jnp.float32)
    rows = inputs.shape[0]
    combined = combined.reshape(rows, -1, HEADS_PER_GROUP + 2, HEAD_SIZE)
    if turning is None:
        turning = angles(positions)
    turning = turning[:, None, None, :]
    query_vectors = rotate(combined[:, :, :HEADS_PER_GROUP], turning).astype(jnp.bfloat16)
    block_keys = rotate(combined[:, :, HEADS_PER_GROUP : HEADS_PER_GROUP + 1], turning)[
        :, :, 0
    ].astype(jnp.bfloat16)
    block_values = combined[:, :, HEADS_PER_GROUP + 1].astype(jnp.bfloat16)
    return (
        query_vectors.reshape(rows, -1),
        block_keys.reshape(rows, -1),
        block_values.reshape(rows, -1),
    )


def attention_kernel(q_ref, kb_ref, vb_ref, us_ref, pg_ref, o_ref, s_ref):
    factor = 1.0 / math.sqrt(HEAD_SIZE)
    nt = (((1,), (1,)), ((), ()))
    q = q_ref[...]
    sb = lax.dot_general(q, kb_ref[...], nt, preferred_element_type=jnp.float32) * factor
    high = jnp.max(sb, axis=1, keepdims=True)
    sources = pg_ref.shape[0]
    chunk = PAGE_ROWS
    for c in range(sources):
        lo = c * chunk
        k = pg_ref[c, 0:chunk, 0:HEAD_SIZE]
        sc = lax.dot_general(q, k, nt, preferred_element_type=jnp.float32) * factor
        sc = jnp.where(us_ref[:, lo : lo + chunk] > 0, sc, -1e30)
        s_ref[:, lo : lo + chunk] = sc
        high = jnp.maximum(high, jnp.max(sc, axis=1, keepdims=True))
    eb = jnp.exp(sb - high)
    tot = jnp.sum(eb, axis=1, keepdims=True)
    acc = jnp.dot(eb.astype(jnp.bfloat16), vb_ref[...], preferred_element_type=jnp.float32)
    for c in range(sources):
        lo = c * chunk
        e = jnp.exp(s_ref[:, lo : lo + chunk] - high)
        tot = tot + jnp.sum(e, axis=1, keepdims=True)
        v = pg_ref[c, 0:chunk, HEAD_SIZE : 2 * HEAD_SIZE]
        acc = acc + jnp.dot(e.astype(jnp.bfloat16), v, preferred_element_type=jnp.float32)
    o_ref[...] = (acc / tot).astype(jnp.bfloat16)


def attend_one(q, kb, vb, pages, usable):
    rows = q.shape[0]
    keys_total = usable.shape[1]
    qspec = pl.BlockSpec((rows, HEAD_SIZE), lambda j: (0, j))
    full = pl.BlockSpec((rows, HEAD_SIZE), lambda j: (0, 0))
    return pl.pallas_call(
        attention_kernel,
        grid=(HEADS_PER_GROUP,),
        in_specs=[
            qspec,
            full,
            full,
            pl.BlockSpec((1, keys_total), lambda j: (0, 0)),
            pl.BlockSpec(pages.shape, lambda j: (0, 0, 0)),
        ],
        out_specs=qspec,
        out_shape=jax.ShapeDtypeStruct(q.shape, jnp.bfloat16),
        scratch_shapes=[pltpu.VMEM((rows, keys_total), jnp.float32)],
        compiler_params=pltpu.CompilerParams(vmem_limit_bytes=48 * 1024 * 1024),
    )(q, kb, vb, usable, pages)


def body(
    embeddings,
    norm_gain,
    query_key_value_weight,
    embed_table,
    rotated_cache_pages,
    page_owner_device,
    cached_length,
    vocab_shard,
    shard_row,
    accept,
):
    members = lax.axis_size("tok")
    length = embeddings.shape[0]
    sources = jnp.arange(members, dtype=jnp.int32)
    positions = cached_length[0] + jnp.arange(length, dtype=jnp.int32)

    own_rows, own_gain, own_turning = lax.optimization_barrier(
        (embeddings, norm_gain, angles(positions))
    )
    query_vectors, block_keys, block_values = lax.optimization_barrier(
        project(own_rows, own_gain, query_key_value_weight, None, own_turning)
    )
    target_shard = vocab_shard[:, 0]
    capacity = max(2, 2 * length // members)
    chosen = (target_shard[:, None] == sources[None, :]).astype(jnp.int32)
    earlier = (jnp.arange(length)[:, None] > jnp.arange(length)[None, :]).astype(jnp.int32)
    slot_rank = jnp.sum(jnp.dot(earlier, chosen) * chosen, axis=1)
    slot_of = target_shard * capacity + slot_rank
    slots = jnp.arange(members * capacity, dtype=jnp.int32)
    wanted = jnp.sum(
        jnp.where(slot_of[:, None] == slots[None, :], shard_row[:, None], 0), axis=0
    ).reshape(members, capacity)
    lanes = rotated_cache_pages.shape[3]
    coded = jnp.concatenate([wanted // ID_SPLIT, wanted % ID_SPLIT], axis=1).astype(jnp.bfloat16)
    coded = jnp.pad(coded, ((0, 0), (0, lanes - coded.shape[1])))
    coded = jnp.broadcast_to(coded[:, None, :], (members, ID_ROWS, lanes))
    outgoing = jnp.concatenate([rotated_cache_pages[0], coded], axis=1)[None]
    arrived = lax.all_to_all(outgoing, "tok", split_axis=1, concat_axis=0, tiled=True)[:, 0]
    page_size = rotated_cache_pages.shape[2]
    ids_in = arrived[:, page_size, : 2 * capacity].astype(jnp.int32)
    asked = ids_in[:, :capacity] * ID_SPLIT + ids_in[:, capacity:]

    page_index = jnp.sum(
        jnp.where(page_owner_device[0][:, None] == sources[None, :], sources[:, None], 0), axis=0
    )
    page_spots = page_index[:, None] * page_size + jnp.arange(page_size, dtype=jnp.int32)[None, :]
    usable = (page_spots.reshape(1, -1) < cached_length[0]).astype(jnp.float32)

    output_one = attend_one(query_vectors, block_keys, block_values, arrived, usable)
    found_rows = jnp.take(embed_table, asked, axis=0)
    returned = lax.all_to_all(found_rows, "tok", split_axis=0, concat_axis=0, tiled=True)
    taken = accept == 1
    most = members
    order = jnp.cumsum(taken.astype(jnp.int32)) - 1
    compact_slots = jnp.arange(most, dtype=jnp.int32)
    hit = taken[:, None] & (order[:, None] == compact_slots[None, :])
    token_of = jnp.sum(jnp.where(hit, jnp.arange(length, dtype=jnp.int32)[:, None], 0), axis=0)
    compact = returned[target_shard[token_of], slot_rank[token_of]]
    full_rows = lax.all_gather(compact, "head", axis=1, tiled=True)
    picked = jnp.take(full_rows, jnp.clip(order, 0, most - 1), axis=0)
    replaced = jnp.where(taken[:, None], picked, embeddings)
    queries_two, keys_two, values_two = project(
        replaced, norm_gain, query_key_value_weight, positions
    )
    output_two = attend_one(queries_two, keys_two, values_two, arrived, usable)
    return output_one, output_two


def solution(mesh):
    return jax.shard_map(
        body,
        mesh=mesh,
        in_specs=(
            P("tok", None),
            P(),
            P(None, "head"),
            P("tok", "head"),
            P("tok", None, None, "head"),
            P("tok", None),
            P("tok"),
            P("tok", None),
            P("tok"),
            P("tok"),
        ),
        out_specs=(P("tok", "head"), P("tok", "head")),
        check_vma=False,
    )
```

time: 170 us -> 182 us (1.071); the launches traced: 170 us -> 179 us
  blocking collectives: 34.2 us -> 13 us
  starting transfers between devices: 6.99 us -> 20.4 us
  between operations: 14.9 us -> 1.71 us
  other arithmetic: 5.62 us -> 16 us
  local copies, waits for them, and re-layouts: 5.67 us -> 13.4 us
  waiting for transfers between devices: 72.8 us -> 79.3 us
  Pallas kernels: 17.8 us -> 23.6 us
    all_to_all x2 -> x0, blocking collectives: 34.2 us -> none  [the longest x1 19.1 us: body(): lax.all_to_all(wanted, 'tok', split_axis=0, concat_axis=0, tiled=True)]
    all_to_all x1 -> x2, waiting for transfers between devices: 47.7 us -> 79.3 us  [the longest x1 79.3 us: body(): lax.all_to_all(outgoing, 'tok', split_axis=1, concat_axis=0, tiled=True)]
    all_gather x1 -> x0, waiting for transfers between devices: 25 us -> none  [body(): full_rows = lax.all_gather(replacement, 'head', axis=1, tiled=True)]
    all_to_all x1 -> x2, starting transfers between devices: 6.77 us -> 20.4 us  [the longest x1 11.8 us: body(): lax.all_to_all(outgoing, 'tok', split_axis=1, concat_axis=0, tiled=True)]
    all_gather x0 -> x1, blocking collectives: none -> 13 us  [body(): full_rows = lax.all_gather(compact, 'head', axis=1, tiled=True)]
    pallas_call x1 -> x2, Pallas kernels: 17.8 us -> 23.6 us  [attend_one(): pl.pallas_call(attention_kernel, grid=(HEADS_PER_GROUP,), in_specs=[qspec...]
    broadcast_in_dim x0 -> x1, other arithmetic: none -> 4.56 us  [body(): outgoing = jnp.concatenate([rotated_cache_pages[0], coded], axis=1)[None]]
    gather x1 -> x4, local copies, waits for them, and re-layouts: 1.95 us -> 6.36 us  [the longest x3 4.19 us: body(): compact = returned[target_shard[token_of], slot_rank[token_of]]]
  transfers between devices with their start and end apart: 2 -> 2, of which waited for: 2 -> 1; matrix products, arithmetic and copies ran while one was open for 10% -> 10% of each run, Pallas kernels for 0% -> 7%
where the time goes in v4:
time: 182 us; the launch traced here: 179 us
  waiting for transfers between devices  79.3 us (44%)
  Pallas kernels  23.6 us (13%)
  starting transfers between devices  20.4 us (11%)
  other arithmetic  16 us (9%)
  local copies, waits for them, and re-layouts  13.4 us (7%)
  blocking collectives  13 us (7%)
  matrix products  11.8 us (6%)
    all_to_all x1, waiting for transfers between devices, body(): lax.all_to_all(outgoing, 'tok', split_axis=1, concat_axis=0, tiled=True)  79.3 us
    pallas_call x2, Pallas kernels, attend_one(): pl.pallas_call(attention_kernel, grid=(HEADS_PER_GROUP,), in_specs=[qspec...  23.6 us
    all_gather x1, blocking collectives, body(): full_rows = lax.all_gather(compact, 'head', axis=1, tiled=True)  13 us
    all_to_all x1, starting transfers between devices, body(): lax.all_to_all(outgoing, 'tok', split_axis=1, concat_axis=0, tiled=True)  11.8 us
    dot_general x2, matrix products, project(): jnp.dot(normed, query_key_value_weight, preferred_element_type=jnp.float32)  10.8 us
    all_to_all x1, starting transfers between devices, body(): lax.all_to_all(found_rows, 'tok', split_axis=0, concat_axis=0, tiled=True)  8.64 us
    broadcast_in_dim x1, other arithmetic, body(): outgoing = jnp.concatenate([rotated_cache_pages[0], coded], axis=1)[None]  4.56 us
    gather x3, local copies, waits for them, and re-layouts, body(): compact = returned[target_shard[token_of], slot_rank[token_of]]  4.19 us
  transfers between devices with their start and end apart: 2, of which 1 were waited for; matrix products, arithmetic and copies ran while one was open for 10% of the time, Pallas kernels for 7%

profile of v4, /device:TPU:28, one launch (start us, length us, event | category | flops | bytes accessed | tf_op | source)
XLA Modules:
  0.0 179.2 jit_solution(7572694472159436447)
XLA Ops:
  0.6 0.0 copy-start
  0.6 1.0 fusion.6
  1.6 0.7 fusion.43
  2.3 0.8 select_reduce_fusion
  3.1 0.1 reshape.319
  3.2 0.1 fusion.32
  3.3 4.6 %maximum_bitcast_fusion = bf16[1,32,264,256]{3,2,0,1:T(8,128)(2,1)} fusion(bf16[32,8,256]{2,1,0:T(8,128)(2,1)S(1)} %broadcast_in_dim.72, bf16[32,256,256]{2,1,0:T(8,128)(2,1)} %bitcast.78), kind=kLoop, calls=%fused_computation.5 | loop fusion | flops 8650752 | bytes 8650752 | tf_op jit(solution)/shard_map/broadcast_in_dim | solution.py:148
  7.9 0.0 copy-start.2
  7.9 11.8 %all-to-all-start = ((bf16[1,32,264,256]{3,2,0,1:T(8,128)(2,1)}), bf16[1,32,264,256]{3,2,0,1:T(8,128)(2,1)}, u32[]{:S(2)}, u32[]{:S(2)}) async-start(bf16[1,32,264,256]{3,2,0,1:T(8,128)(2,1)} %maximum_bitcast_fusion), calls=%async_computation | async-start | bytes 8650752 | tf_op jit(solution)/shard_map/all_to_all | solution.py:149
  19.7 0.0 copy-done.14
  19.7 0.0 copy-start.11
  19.7 0.1 copy.65
  19.8 0.2 reduce-window.4
  20.0 0.7 fusion.23
  20.7 0.1 select_reduce_fusion.1
  20.8 1.2 gather_fusion.2
  22.1 0.0 copy-done.1
  22.1 1.3 gather_fusion.1
  23.4 0.0 copy-done.6
  24.1 0.3 multiply_cosine_fusion.1
  24.4 0.7 copy.67
  25.1 0.7 copy.68
  25.8 0.1 select_reduce_fusion.2
  25.9 0.1 convert_bitcast_fusion
  26.0 0.0 copy-done.2
  26.0 0.3 fusion
  26.3 5.4 %fusion.9 = f32[128,768]{0,1:T(8,128)S(1)} fusion(bf16[4096,768]{1,0:T(8,128)(2,1)} %param.12, bf16[128,4096]{1,0:T(8,128)(2,1)S(1)} %copy-done.2, f32[4096]{0:T(1024)S(1)} %convert_element_type.87, f32[128]{0:T(128)S(1)} %add_rsqrt_fusion.1), kind=kOutput, calls=%fused_computation.19 | convolution fusion | flops 807403520 | bytes 7750144 | tf_op jit(solution)/shard_map/dot_general | solution.py:44
  31.7 0.7 slice.80
  32.4 0.1 copy-done.3
  32.5 0.1 copy.76
  32.6 0.1 copy.77
  32.7 0.2 fusion.47
  32.9 0.1 copy.59
  33.0 0.7 copy.60
  33.7 0.9 copy.78
  34.6 0.1 maximum_bitcast_fusion.1.kb_ref
  34.7 1.0 subtract_convert_fusion.1
  35.8 0.1 copy.64.q_ref
  35.9 79.3 %all-to-all-done = bf16[1,32,264,256]{3,2,0,1:T(8,128)(2,1)} async-done(((bf16[1,32,264,256]{3,2,0,1:T(8,128)(2,1)}), bf16[1,32,264,256]{3,2,0,1:T(8,128)(2,1)}, u32[]{:S(2)}, u32[]{:S(2)}) %all-to-all-start) | async-done | bytes 4325408 | tf_op jit(solution)/shard_map/all_to_all | solution.py:149
  115.2 0.9 slice_convert_fusion
  116.1 0.1 compare_and_fusion
  116.2 0.1 reshape.327
  116.3 1.9 %gather_fusion = bf16[256,512]{1,0:T(8,128)(2,1)} fusion(bf16[2048,512]{1,0:T(8,128)(2,1)S(1)} %copy-done, s32[1024]{0:T(1024)S(1)} %pad_clamp_fusion.2), kind=kCustom, calls=%fused_computation | custom fusion | bytes 525312 | tf_op jit(solution)/shard_map/jit(_take)/gather | solution.py:161
  118.1 1.8 bitcast_select_fusion
  119.9 8.6 %all-to-all-start.1 = ((bf16[32,8,512]{2,1,0:T(8,128)(2,1)}), bf16[32,8,512]{2,1,0:T(8,128)(2,1)}, u32[]{:S(2)}, u32[]{:S(2)}) async-start(bf16[32,8,512]{2,1,0:T(8,128)(2,1)} %bitcast_select_fusion), calls=%async_computation.1 | async-start | bytes 524288 | tf_op jit(solution)/shard_map/all_to_all | solution.py:162
  128.6 0.7 pad_clamp_fusion
  129.2 0.6 compare_and_fusion.1
  129.9 0.7 fusion.44
  130.5 11.8 %shard_map.113 = bf16[128,512]{1,0:T(8,128)(2,1)} custom-call(bf16[128,512]{1,0:T(8,128)(2,1)S(1)} %copy.64.q_ref, bf16[128,128]{1,0:T(8,128)(2,1)S(1)} %maximum_bitcast_fusion.1.kb_ref, bf16[128,128]{1,0:T(8,128)(2,1)S(1)} %bitcast.74, f32[1,8192]{1,0:T(1,128)S(1)} %bitcast.72, bf16[32,264,256]{2,1,0:T(8,128)(2,1)} %bitcast.13.pg_ref), custom_call_target="tpu_custom_call" | custom-call | tf_op jit(solution)/shard_map/pallas_call | solution.py:94
  142.3 0.0 all-to-all-done.1
  142.3 1.7 gather_fusion.3
  144.0 13.0 %all_gather.3 = bf16[32,4096]{1,0:T(8,128)(2,1)S(1)} all-gather(bf16[32,512]{1,0:T(8,128)(2,1)S(1)} %gather_fusion.3), channel_id=1, replica_groups=mesh['tok'=32,'head'=8] {'head'}, dimensions={1}, use_global_device_ids=true | all-gather | bytes 294912 | tf_op jit(solution)/shard_map/all_gather | solution.py:170
  157.0 2.2 %gather_fusion.4 = bf16[128,4096]{1,0:T(8,128)(2,1)} fusion(bf16[32,4096]{1,0:T(8,128)(2,1)S(1)} %all_gather.3, s32[1024]{0:T(1024)S(1)} %pad_clamp_fusion), kind=kCustom, calls=%fused_computation.4 | custom fusion | bytes 2097664 | tf_op jit(solution)/shard_map/jit(_take)/gather | solution.py:171
  159.2 0.0 copy-done.12
  159.2 1.8 %fusion.3 = (f32[128]{0:T(128)S(1)}, bf16[128,4096]{1,0:T(8,128)(2,1)S(1)}) fusion(bf16[128,4096]{1,0:T(8,128)(2,1)S(1)} %copy-done.2, bf16[128,4096]{1,0:T(8,128)(2,1)} %gather_fusion.4, pred[128]{0:T(512)(128)(4,1)S(1)} %compare_and_fusion.1, pred[128]{0:T(512)(128)(4,1)S(1)} %copy-done.12), kind=kLoop, calls=%fused_computation.13 | loop fusion | flops 2621312 | bytes 3146496 | tf_op jit(solution)/shard_map/reduce_sum | solution.py:42
  161.0 0.0 copy-start.8
  161.1 5.4 %fusion.7 = f32[128,768]{0,1:T(8,128)S(1)} fusion(bf16[4096,768]{1,0:T(8,128)(2,1)} %param.12, bf16[128,4096]{1,0:T(8,128)(2,1)S(1)} %get-tuple-element.17, f32[4096]{0:T(1024)S(1)} %convert_element_type.97, f32[128]{0:T(128)S(1)} %add_rsqrt_fusion), kind=kOutput, calls=%fused_computation.18 | convolution fusion | flops 807403520 | bytes 7750144 | tf_op jit(solution)/shard_map/dot_general | solution.py:44
  166.5 0.1 copy.79
  166.6 0.1 copy.80
  166.8 0.1 copy.73.q_ref
  166.9 0.1 copy.81
  167.0 0.3 fusion.20
  167.4 0.1 maximum_bitcast_fusion.2.kb_ref
  167.5 11.8 %shard_map.114 = bf16[128,512]{1,0:T(8,128)(2,1)} custom-call(bf16[128,512]{1,0:T(8,128)(2,1)S(1)} %copy.73.q_ref, bf16[128,128]{1,0:T(8,128)(2,1)S(1)} %maximum_bitcast_fusion.2.kb_ref, bf16[128,128]{1,0:T(8,128)(2,1)S(1)} %bitcast.75, f32[1,8192]{1,0:T(1,128)S(1)} %bitcast.73, bf16[32,264,256]{2,1,0:T(8,128)(2,1)} %bitcast.13.pg_ref), custom_call_target="tpu_custom_call" | custom-call | tf_op jit(solution)/shard_map/pallas_call | solution.py:94
  (43 shorter events, 0.3 us)
Async XLA Ops:
  0.6 115.6 %copy-start = (bf16[2048,512]{1,0:T(8,128)(2,1)S(1)}, bf16[2048,512]{1,0:T(8,128)(2,1)}, u32[]{:S(2)}) copy-start(bf16[2048,512]{1,0:T(8,128)(2,1)} %param.13) | copy-start | bytes 6291460
  7.9 11.8 %copy-start.14 = (s32[128]{0:T(128)S(1)}, s32[128]{0:T(128)}, u32[]{:S(2)}) copy-start(s32[128]{0:T(128)} %param.19) | copy-start | bytes 1540
  7.9 14.2 %copy-start.1 = (s32[128,1]{0,1:T(1,128)S(1)}, s32[128,1]{0,1:T(1,128)}, u32[]{:S(2)}) copy-start(s32[128,1]{0,1:T(1,128)} %param.17) | copy-start | bytes 1540
  7.9 15.5 %copy-start.6 = (bf16[4096]{0:T(1024)(128)(2,1)S(1)}, bf16[4096]{0:T(1024)(128)(2,1)}, u32[]{:S(2)}) copy-start(bf16[4096]{0:T(1024)(128)(2,1)} %param.11) | copy-start | bytes 24580
  7.9 17.9 %copy-start.15 = (s32[1,32]{1,0:T(1,128)S(1)}, s32[1,32]{1,0:T(1,128)}, u32[]{:S(2)}) copy-start(s32[1,32]{1,0:T(1,128)} %param.15) | copy-start | bytes 388
  7.9 18.1 %copy-start.2 = (bf16[128,4096]{1,0:T(8,128)(2,1)S(1)}, bf16[128,4096]{1,0:T(8,128)(2,1)}, u32[]{:S(2)}) copy-start(bf16[128,4096]{1,0:T(8,128)(2,1)} %param.10) | copy-start | bytes 3145732
  7.9 107.3 %all-to-all-start = ((bf16[1,32,264,256]{3,2,0,1:T(8,128)(2,1)}), bf16[1,32,264,256]{3,2,0,1:T(8,128)(2,1)}, u32[]{:S(2)}, u32[]{:S(2)}) async-start(bf16[1,32,264,256]{3,2,0,1:T(8,128)(2,1)} %maximum_bitcast_fusion), calls=%async_computation | async-start | bytes 8650752 | tf_op jit(solution)/shard_map/all_to_all | solution.py:149
  19.7 1.1 copy-start.11
  20.7 5.2 %copy-start.13 = (s32[128]{0:T(128)}, s32[128]{0:T(128)S(1)}, u32[]{:S(2)}) copy-start(s32[128]{0:T(128)S(1)} %get-tuple-element.15) | copy-start | bytes 1540
  24.0 7.7 %copy-start.7 = (f32[64]{0:T(128)}, f32[64]{0:T(128)S(1)}, u32[]{:S(2)}) copy-start(f32[64]{0:T(128)S(1)} %multiply_power_fusion) | copy-start | bytes 772
  24.1 7.7 %copy-start.9 = (f32[128]{0:T(128)}, f32[128]{0:T(128)S(1)}, u32[]{:S(2)}) copy-start(f32[128]{0:T(128)S(1)} %add_convert_fusion.2) | copy-start | bytes 1540
  31.7 0.8 copy-start.3
  119.9 22.4 %all-to-all-start.1 = ((bf16[32,8,512]{2,1,0:T(8,128)(2,1)}), bf16[32,8,512]{2,1,0:T(8,128)(2,1)}, u32[]{:S(2)}, u32[]{:S(2)}) async-start(bf16[32,8,512]{2,1,0:T(8,128)(2,1)} %bitcast_select_fusion), calls=%async_computation.1 | async-start | bytes 524288 | tf_op jit(solution)/shard_map/all_to_all | solution.py:162
  157.0 2.2 %copy-start.12 = (pred[128]{0:T(512)(128)(4,1)S(1)}, pred[128]{0:T(512)(128)(4,1)}, u32[]{:S(2)}) copy-start(pred[128]{0:T(512)(128)(4,1)} %copy-done.11) | copy-start | bytes 388
  161.0 5.7 %copy-start.4 = (f32[128,64]{0,1:T(8,128)S(1)}, f32[128,64]{0,1:T(8,128)}, u32[]{:S(2)}) copy-start(f32[128,64]{0,1:T(8,128)} %copy.67) | copy-start | bytes 98308
  161.0 5.7 %copy-start.5 = (f32[128,64]{0,1:T(8,128)S(1)}, f32[128,64]{0,1:T(8,128)}, u32[]{:S(2)}) copy-start(f32[128,64]{0,1:T(8,128)} %copy.68) | copy-start | bytes 98308
  161.0 6.0 %copy-start.8 = (f32[64]{0:T(128)S(1)}, f32[64]{0:T(128)}, u32[]{:S(2)}) copy-start(f32[64]{0:T(128)} %copy-done.7) | copy-start | bytes 772
  161.0 6.0 %copy-start.10 = (f32[128]{0:T(128)S(1)}, f32[128]{0:T(128)}, u32[]{:S(2)}) copy-start(f32[128]{0:T(128)} %copy-done.9) | copy-start | bytes 1540
